TPU v7x, 32 devices: a whole 2x2x4 slice. The times are simulated.
32 devices in a mesh: dp: 4 (over z), ctx: 2 (over y), seq: 4 (over x, core).
Axes of the slice: x: 2, y: 2, z: 4, core: 2. Of those that a mesh axis runs over, the one named last changes fastest.
Arguments:
- layer_input: bfloat16 [16, 1024, 768], P('dp', ('ctx', 'seq')), may hold values from -6 to 6
- block_order: int32 [16, 8], P('dp'), may hold values from 0 to 7, each once within a row
- attn_gain: bfloat16 [768], P(('dp', 'ctx')), may hold values from 0.3984375 to 1.59375
- attn_shift: bfloat16 [768], P(('dp', 'ctx')), may hold values from -3 to 3
- w_qkv: bfloat16 [768, 2304], P(('dp', 'ctx')), may hold values from -0.21875 to 0.21875
- bias_query: bfloat16 [768], P(('dp', 'ctx')), may hold values from -3 to 3
- bias_value: bfloat16 [768], P(('dp', 'ctx')), may hold values from -3 to 3
- w_out: bfloat16 [768, 768], P(('dp', 'ctx')), may hold values from -3 to 3
- bias_out: bfloat16 [768], P(('dp', 'ctx')), may hold values from -3 to 3
- mlp_gain: bfloat16 [768], P(('dp', 'ctx')), may hold values from 0.3984375 to 1.59375
- mlp_shift: bfloat16 [768], P(('dp', 'ctx')), may hold values from -3 to 3
- w_up: bfloat16 [768, 3072], P(('dp', 'ctx')), may hold values from -0.21875 to 0.21875
- bias_up: bfloat16 [3072], P(('dp', 'ctx')), may hold values from -3 to 3
- w_down: bfloat16 [3072, 768], P(('dp', 'ctx')), may hold values from -0.109375 to 0.109375
- bias_down: bfloat16 [768], P(('dp', 'ctx')), may hold values from -3 to 3
- cotangent: bfloat16 [16, 1024, 768], P('dp', ('ctx', 'seq')), may hold values from -6 to 6
Outputs:
- layer_output: bfloat16 [16, 1024, 768], P('dp', ('ctx', 'seq'))
- grad_input: bfloat16 [16, 1024, 768], P('dp', ('ctx', 'seq'))
- grad_attn_gain: float32 [768], P(('dp', 'ctx'))
- grad_attn_shift: float32 [768], P(('dp', 'ctx'))
- grad_w_qkv: float32 [768, 2304], P(('dp', 'ctx'))
- grad_bias_query: float32 [768], P(('dp', 'ctx'))
- grad_bias_value: float32 [768], P(('dp', 'ctx'))
- grad_w_out: float32 [768, 768], P(('dp', 'ctx'))
- grad_bias_out: float32 [768], P(('dp', 'ctx'))
- grad_mlp_gain: float32 [768], P(('dp', 'ctx'))
- grad_mlp_shift: float32 [768], P(('dp', 'ctx'))
- grad_w_up: float32 [768, 3072], P(('dp', 'ctx'))
- grad_bias_up: float32 [3072], P(('dp', 'ctx'))
- grad_w_down: float32 [3072, 768], P(('dp', 'ctx'))
- grad_bias_down: float32 [768], P(('dp', 'ctx'))
Inputs may be any that keep to these rules, and one draw needn't show every extreme that they name: Each row of block_order names every block number 0 to 7 once.
All inputs are finite; a program needn't handle non-finite values.
Results may differ from a plain program's by a relative error of at most 0.035.
Values may be sent and summed in bfloat16 or wider, within the bound.
No kernel may reach another device: no remote copies, remote signals or barrier semaphores. Data moves between devices by JAX's collectives and lax.ppermute only.
A program may use at most 192 MiB of HBM per device.

v0:
```python
import jax
import jax.numpy as jnp
from jax import lax
from jax.sharding import PartitionSpec as P

HEAD_DIM = 64


NEG_BIG = -1e30


def layer_norm(values, gain_vec, shift_vec):
    row_mean = jnp.mean(values, axis=-1, keepdims=True)
    centred = values - row_mean
    row_var = jnp.mean(centred * centred, axis=-1, keepdims=True)
    return centred * lax.rsqrt(row_var + 1e-05) * gain_vec + shift_vec


def gelu_tanh(up_in):
    return (
        0.5
        * up_in
        * (1.0 + jnp.tanh(0.7978845608028654 * (up_in + 0.044715 * up_in * up_in * up_in)))
    )


def block_loop(row_count, step_fn, running):
    block_size = 512
    block_count = row_count // block_size
    return lax.fori_loop(
        0,
        block_count,
        lambda block_index, state_now: step_fn(state_now, block_index * block_size, block_size),
        running,
    )


def local(
    layer_input,
    block_order,
    attn_gain,
    attn_shift,
    w_qkv,
    bias_query,
    bias_value,
    w_out,
    bias_out,
    mlp_gain,
    mlp_shift,
    w_up,
    bias_up,
    w_down,
    bias_down,
    cotangent,
):
    f32 = jnp.float32
    bf16 = jnp.bfloat16
    shards = (
        attn_gain,
        attn_shift,
        w_qkv,
        bias_query,
        bias_value,
        w_out,
        bias_out,
        mlp_gain,
        mlp_shift,
        w_up,
        bias_up,
        w_down,
        bias_down,
    )
    whole = (
        lax.all_gather(shards[0], ("dp", "ctx"), axis=0, tiled=True),
        lax.all_gather(shards[1], ("dp", "ctx"), axis=0, tiled=True),
        lax.all_gather(shards[2], ("dp", "ctx"), axis=0, tiled=True),
        lax.all_gather(shards[3], ("dp", "ctx"), axis=0, tiled=True),
        lax.all_gather(shards[4], ("dp", "ctx"), axis=0, tiled=True),
        lax.all_gather(shards[5], ("dp", "ctx"), axis=0, tiled=True),
        lax.all_gather(shards[6], ("dp", "ctx"), axis=0, tiled=True),
        lax.all_gather(shards[7], ("dp", "ctx"), axis=0, tiled=True),
        lax.all_gather(shards[8], ("dp", "ctx"), axis=0, tiled=True),
        lax.all_gather(shards[9], ("dp", "ctx"), axis=0, tiled=True),
        lax.all_gather(shards[10], ("dp", "ctx"), axis=0, tiled=True),
        lax.all_gather(shards[11], ("dp", "ctx"), axis=0, tiled=True),
        lax.all_gather(shards[12], ("dp", "ctx"), axis=0, tiled=True),
    )
    (
        whole_attn_gain,
        whole_attn_shift,
        whole_w_qkv,
        whole_bias_query,
        whole_bias_value,
        whole_w_out,
        whole_bias_out,
        whole_mlp_gain,
        whole_mlp_shift,
        whole_w_up,
        whole_bias_up,
        whole_w_down,
        whole_bias_down,
    ) = whole
    seq_count, seg_len, model_width = layer_input.shape
    seq_devices = lax.axis_size("seq")
    head_width = model_width // seq_devices
    head_groups = head_width // HEAD_DIM
    ctx_span = seg_len * seq_devices
    scaling = HEAD_DIM ** (-0.5)
    all_pos = jnp.repeat(block_order, seg_len, axis=1) * seg_len + jnp.tile(
        jnp.arange(seg_len, dtype=jnp.int32), block_order.shape[1]
    )
    query_pos = lax.dynamic_slice_in_dim(all_pos, lax.axis_index("ctx") * ctx_span, ctx_span, 1)
    input_f32 = layer_input.astype(f32)
    normed_a, pull_attn = jax.vjp(
        layer_norm, input_f32, whole_attn_gain.astype(f32), whole_attn_shift.astype(f32)
    )
    normed_ab = normed_a.astype(bf16)
    qkv_bias = jnp.concatenate(
        [whole_bias_query, jnp.zeros_like(whole_bias_query), whole_bias_value]
    ).astype(f32)
    qkv_pre = jnp.dot(normed_ab, whole_w_qkv, preferred_element_type=f32) + qkv_bias
    qkv_tok = qkv_pre.astype(bf16).reshape(seq_count, seg_len, 3, model_width)
    qkv_heads = lax.all_to_all(qkv_tok, "seq", split_axis=3, concat_axis=1, tiled=True)
    head_shape = (seq_count, ctx_span, head_groups, HEAD_DIM)
    queries = qkv_heads[:, :, 0].reshape(head_shape)
    key_rows = qkv_heads[:, :, 1].reshape(head_shape)
    value_rows = qkv_heads[:, :, 2].reshape(head_shape)
    stat_shape = (seq_count, ctx_span, head_groups)
    start_state = (
        jnp.full(stat_shape, NEG_BIG, f32),
        jnp.zeros(stat_shape, f32),
        jnp.zeros(head_shape, f32),
    )
    key_piece = lax.all_gather(key_rows, "ctx", axis=1, tiled=True)
    value_piece = lax.all_gather(value_rows, "ctx", axis=1, tiled=True)

    def step_fn(state_now, offset, block_size):
        run_max, denominator, accumulated = state_now
        key_block = lax.dynamic_slice_in_dim(key_piece, offset, block_size, 1)
        value_block = lax.dynamic_slice_in_dim(value_piece, offset, block_size, 1)
        key_pos = lax.dynamic_slice_in_dim(all_pos, offset, block_size, 1)
        scores = (
            jnp.einsum("nqhd,nkhd->nqhk", queries, key_block, preferred_element_type=f32) * scaling
        )
        visible = key_pos[:, None, None, :] <= query_pos[:, :, None, None]
        new_max = jnp.maximum(run_max, jnp.max(jnp.where(visible, scores, NEG_BIG), axis=-1))
        correction = jnp.exp(run_max - new_max)
        weights_p = jnp.where(visible, jnp.exp(scores - new_max[..., None]), 0.0)
        denominator = denominator * correction + jnp.sum(weights_p, axis=-1)
        accumulated = accumulated * correction[..., None] + jnp.einsum(
            "nqhk,nkhd->nqhd", weights_p.astype(bf16), value_block, preferred_element_type=f32
        )
        return (new_max, denominator, accumulated)

    run_max, denominator, accumulated = block_loop(key_piece.shape[1], step_fn, start_state)
    log_sum = run_max + jnp.log(denominator)
    attn_out = accumulated / denominator[..., None]
    ctx_heads = attn_out.reshape(seq_count, ctx_span, head_width).astype(bf16)
    context = lax.all_to_all(ctx_heads, "seq", split_axis=1, concat_axis=2, tiled=True)
    hidden = (
        input_f32
        + jnp.dot(context, whole_w_out, preferred_element_type=f32)
        + whole_bias_out.astype(f32)
    )
    normed_m, pull_mlp = jax.vjp(
        layer_norm, hidden, whole_mlp_gain.astype(f32), whole_mlp_shift.astype(f32)
    )
    normed_mb = normed_m.astype(bf16)
    up_in = jnp.dot(normed_mb, whole_w_up, preferred_element_type=f32) + whole_bias_up.astype(f32)
    active, pull_gelu = jax.vjp(gelu_tanh, up_in)
    active_b = active.astype(bf16)
    layer_output = (
        hidden
        + jnp.dot(active_b, whole_w_down, preferred_element_type=f32)
        + whole_bias_down.astype(f32)
    ).astype(bf16)
    again = (
        lax.all_gather(shards[0], ("dp", "ctx"), axis=0, tiled=True),
        lax.all_gather(shards[1], ("dp", "ctx"), axis=0, tiled=True),
        lax.all_gather(shards[2], ("dp", "ctx"), axis=0, tiled=True),
        lax.all_gather(shards[3], ("dp", "ctx"), axis=0, tiled=True),
        lax.all_gather(shards[4], ("dp", "ctx"), axis=0, tiled=True),
        lax.all_gather(shards[5], ("dp", "ctx"), axis=0, tiled=True),
        lax.all_gather(shards[6], ("dp", "ctx"), axis=0, tiled=True),
        lax.all_gather(shards[7], ("dp", "ctx"), axis=0, tiled=True),
        lax.all_gather(shards[8], ("dp", "ctx"), axis=0, tiled=True),
        lax.all_gather(shards[9], ("dp", "ctx"), axis=0, tiled=True),
        lax.all_gather(shards[10], ("dp", "ctx"), axis=0, tiled=True),
        lax.all_gather(shards[11], ("dp", "ctx"), axis=0, tiled=True),
        lax.all_gather(shards[12], ("dp", "ctx"), axis=0, tiled=True),
    )
    back_w_qkv = again[2]
    back_w_out = again[5]
    back_w_up = again[9]
    back_w_down = again[11]
    grad_w_down = jnp.einsum("nsf,nsd->fd", active_b, cotangent, preferred_element_type=f32)
    grad_bias_down = jnp.sum(cotangent, axis=(0, 1), dtype=f32)
    grad_active = jnp.einsum("nsd,fd->nsf", cotangent, back_w_down, preferred_element_type=f32)
    (grad_up_f,) = pull_gelu(grad_active)
    grad_up = grad_up_f.astype(bf16)
    grad_w_up = jnp.einsum("nsd,nsf->df", normed_mb, grad_up, preferred_element_type=f32)
    grad_bias_up = jnp.sum(grad_up, axis=(0, 1), dtype=f32)
    grad_normed_m = jnp.einsum("nsf,df->nsd", grad_up, back_w_up, preferred_element_type=f32)
    grad_hidden_norm, grad_mlp_gain, grad_mlp_shift = pull_mlp(grad_normed_m)
    grad_hidden = cotangent.astype(f32) + grad_hidden_norm
    grad_att = grad_hidden.astype(bf16)
    grad_w_out = jnp.einsum("nsc,nsd->cd", context, grad_att, preferred_element_type=f32)
    grad_bias_out = jnp.sum(grad_att, axis=(0, 1), dtype=f32)
    grad_context = jnp.einsum(
        "nsd,cd->nsc", grad_att, back_w_out, preferred_element_type=f32
    ).astype(bf16)
    grad_out_h = lax.all_to_all(
        grad_context, "seq", split_axis=2, concat_axis=1, tiled=True
    ).reshape(head_shape)
    delta = jnp.sum(grad_out_h.astype(f32) * attn_out, axis=-1)

    def query_grads(
        query_block, gradout_block, key_block, value_block, visible, lse_block, delta_block
    ):
        scores = (
            jnp.einsum("nqhd,nkhd->nqhk", query_block, key_block, preferred_element_type=f32)
            * scaling
        )
        probability = jnp.where(visible, jnp.exp(scores - lse_block[..., None]), 0.0)
        grad_prob = jnp.einsum(
            "nqhd,nkhd->nqhk", gradout_block, value_block, preferred_element_type=f32
        )
        grad_scores = (probability * (grad_prob - delta_block[..., None])).astype(bf16)
        return (probability, grad_scores)

    dq_key_piece = lax.all_gather(key_rows, "ctx", axis=1, tiled=True)
    dq_value_piece = lax.all_gather(value_rows, "ctx", axis=1, tiled=True)

    def step_fn(grad_query, offset, block_size):
        key_block = lax.dynamic_slice_in_dim(dq_key_piece, offset, block_size, 1)
        value_block = lax.dynamic_slice_in_dim(dq_value_piece, offset, block_size, 1)
        key_pos = lax.dynamic_slice_in_dim(all_pos, offset, block_size, 1)
        visible = key_pos[:, None, None, :] <= query_pos[:, :, None, None]
        probability, grad_scores = query_grads(
            queries, grad_out_h, key_block, value_block, visible, log_sum, delta
        )
        return (
            grad_query
            + jnp.einsum("nqhk,nkhd->nqhd", grad_scores, key_block, preferred_element_type=f32)
            * scaling
        )

    grad_query = block_loop(dq_key_piece.shape[1], step_fn, jnp.zeros(head_shape, f32))
    gathered_lse, gathered_delta = (
        lax.all_gather(log_sum.astype(jnp.bfloat16), "ctx", axis=1, tiled=True).astype(
            log_sum.dtype
        ),
        lax.all_gather(delta.astype(jnp.bfloat16), "ctx", axis=1, tiled=True).astype(delta.dtype),
    )
    query_piece = lax.all_gather(queries, "ctx", axis=1, tiled=True)
    gradout_piece = lax.all_gather(grad_out_h, "ctx", axis=1, tiled=True)

    def step_fn(state_now, offset, block_size):
        grad_key, grad_value = state_now
        query_block = lax.dynamic_slice_in_dim(query_piece, offset, block_size, 1)
        gradout_block = lax.dynamic_slice_in_dim(gradout_piece, offset, block_size, 1)
        block_pos = lax.dynamic_slice_in_dim(all_pos, offset, block_size, 1)
        lse_block = lax.dynamic_slice_in_dim(gathered_lse, offset, block_size, 1)
        delta_block = lax.dynamic_slice_in_dim(gathered_delta, offset, block_size, 1)
        visible = query_pos[:, None, None, :] <= block_pos[:, :, None, None]
        probability, grad_scores = query_grads(
            query_block, gradout_block, key_rows, value_rows, visible, lse_block, delta_block
        )
        grad_value = grad_value + jnp.einsum(
            "nqhk,nqhd->nkhd", probability.astype(bf16), gradout_block, preferred_element_type=f32
        )
        grad_key = (
            grad_key
            + jnp.einsum("nqhk,nqhd->nkhd", grad_scores, query_block, preferred_element_type=f32)
            * scaling
        )
        return (grad_key, grad_value)

    grad_key, grad_value = block_loop(
        query_piece.shape[1], step_fn, (jnp.zeros(head_shape, f32), jnp.zeros(head_shape, f32))
    )
    flat_shape = (seq_count, ctx_span, head_width)
    grad_qkv_heads = jnp.stack(
        [
            grad_query.astype(bf16).reshape(flat_shape),
            grad_key.astype(bf16).reshape(flat_shape),
            grad_value.astype(bf16).reshape(flat_shape),
        ],
        2,
    )
    grad_qkv = lax.all_to_all(
        grad_qkv_heads, "seq", split_axis=1, concat_axis=3, tiled=True
    ).reshape(seq_count, seg_len, 3 * model_width)
    grad_w_qkv = jnp.einsum("nsd,nsc->dc", normed_ab, grad_qkv, preferred_element_type=f32)
    grad_bias_query = jnp.sum(grad_qkv[:, :, :model_width], axis=(0, 1), dtype=f32)
    grad_bias_value = jnp.sum(grad_qkv[:, :, 2 * model_width :], axis=(0, 1), dtype=f32)
    grad_normed_a = jnp.einsum("nsc,dc->nsd", grad_qkv, back_w_qkv, preferred_element_type=f32)
    grad_input_norm, grad_attn_gain, grad_attn_shift = pull_attn(grad_normed_a)
    grad_input = (grad_hidden + grad_input_norm).astype(bf16)
    grads = (
        grad_attn_gain,
        grad_attn_shift,
        grad_w_qkv,
        grad_bias_query,
        grad_bias_value,
        grad_w_out,
        grad_bias_out,
        grad_mlp_gain,
        grad_mlp_shift,
        grad_w_up,
        grad_bias_up,
        grad_w_down,
        grad_bias_down,
    )
    shares = (
        lax.psum_scatter(grads[0], ("dp", "ctx"), scatter_dimension=0, tiled=True),
        lax.psum_scatter(grads[1], ("dp", "ctx"), scatter_dimension=0, tiled=True),
        lax.psum_scatter(grads[2], ("dp", "ctx"), scatter_dimension=0, tiled=True),
        lax.psum_scatter(grads[3], ("dp", "ctx"), scatter_dimension=0, tiled=True),
        lax.psum_scatter(grads[4], ("dp", "ctx"), scatter_dimension=0, tiled=True),
        lax.psum_scatter(grads[5], ("dp", "ctx"), scatter_dimension=0, tiled=True),
        lax.psum_scatter(grads[6], ("dp", "ctx"), scatter_dimension=0, tiled=True),
        lax.psum_scatter(grads[7], ("dp", "ctx"), scatter_dimension=0, tiled=True),
        lax.psum_scatter(grads[8], ("dp", "ctx"), scatter_dimension=0, tiled=True),
        lax.psum_scatter(grads[9], ("dp", "ctx"), scatter_dimension=0, tiled=True),
        lax.psum_scatter(grads[10], ("dp", "ctx"), scatter_dimension=0, tiled=True),
        lax.psum_scatter(grads[11], ("dp", "ctx"), scatter_dimension=0, tiled=True),
        lax.psum_scatter(grads[12], ("dp", "ctx"), scatter_dimension=0, tiled=True),
    )
    totals = (
        lax.psum(shares[0].astype(jnp.bfloat16), "seq").astype(jnp.float32),
        lax.psum(shares[1].astype(jnp.bfloat16), "seq").astype(jnp.float32),
        lax.psum(shares[2].astype(jnp.bfloat16), "seq").astype(jnp.float32),
        lax.psum(shares[3].astype(jnp.bfloat16), "seq").astype(jnp.float32),
        lax.psum(shares[4].astype(jnp.bfloat16), "seq").astype(jnp.float32),
        lax.psum(shares[5].astype(jnp.bfloat16), "seq").astype(jnp.float32),
        lax.psum(shares[6].astype(jnp.bfloat16), "seq").astype(jnp.float32),
        lax.psum(shares[7].astype(jnp.bfloat16), "seq").astype(jnp.float32),
        lax.psum(shares[8].astype(jnp.bfloat16), "seq").astype(jnp.float32),
        lax.psum(shares[9].astype(jnp.bfloat16), "seq").astype(jnp.float32),
        lax.psum(shares[10].astype(jnp.bfloat16), "seq").astype(jnp.float32),
        lax.psum(shares[11].astype(jnp.bfloat16), "seq").astype(jnp.float32),
        lax.psum(shares[12].astype(jnp.bfloat16), "seq").astype(jnp.float32),
    )
    return (layer_output, grad_input) + tuple(totals)


def solution(mesh):
    placed = (
        P("dp", ("ctx", "seq"), None),
        P("dp", None),
        P(("dp", "ctx")),
        P(("dp", "ctx")),
        P(("dp", "ctx"), None),
        P(("dp", "ctx")),
        P(("dp", "ctx")),
        P(("dp", "ctx"), None),
        P(("dp", "ctx")),
        P(("dp", "ctx")),
        P(("dp", "ctx")),
        P(("dp", "ctx"), None),
        P(("dp", "ctx")),
        P(("dp", "ctx"), None),
        P(("dp", "ctx")),
        P("dp", ("ctx", "seq"), None),
    )
    return jax.shard_map(
        local,
        mesh=mesh,
        in_specs=placed,
        out_specs=(
            P("dp", ("ctx", "seq"), None),
            P("dp", ("ctx", "seq"), None),
            P(("dp", "ctx")),
            P(("dp", "ctx")),
            P(("dp", "ctx"), None),
            P(("dp", "ctx")),
            P(("dp", "ctx")),
            P(("dp", "ctx"), None),
            P(("dp", "ctx")),
            P(("dp", "ctx")),
            P(("dp", "ctx")),
            P(("dp", "ctx"), None),
            P(("dp", "ctx")),
            P(("dp", "ctx"), None),
            P(("dp", "ctx")),
        ),
        check_vma=False,
    )
```

profile of v0, /device:TPU:0, one launch (start us, length us, event | category | flops | bytes accessed | tf_op | source)
XLA Modules:
  0.0 1111.8 jit_solution(2099811588299873904)
XLA Ops:
  16.7 40.5 %all-reduce.18 = (bf16[768]{0:T(1024)(128)(2,1)S(1)}, bf16[768]{0:T(1024)(128)(2,1)S(1)}, bf16[768]{0:T(1024)(128)(2,1)S(1)}, bf16[768]{0:T(1024)(128)(2,1)S(1)}...) all-reduce(bf16[768]{0:T(1024)(128)(2,1)S(1)} %dynamic-update-slice, ...), channel_id=1, replica_groups=mesh['dp'=4,'ctx'=2,'seq'=4] {'dp','ctx'}, use_global_device_ids=true, to_apply=%add.3 | all-reduce | flops 6144 | bytes 24576
  59.5 18.4 %all-gather.10.cloned.1.call-done = bf16[768,2304]{1,0:T(8,128)(2,1)} async-done(((bf16[96,2304]{1,0:T(8,128)(2,1)}), bf16[768,2304]{1,0:T(8,128)(2,1)}) %all-gather.10.cloned.1.call-update) | async-done | bytes 3538960 | tf_op jit(solution)/shard_map/all_gather | solution.py:76
  78.0 5.6 fusion.84
  88.4 31.0 %all_to_all.66 = bf16[4,128,3,768]{1,0,2,3:T(4,128)(2,1)S(1)} all-to-all(bf16[4,128,3,768]{1,0,2,3:T(4,128)(2,1)S(1)} %copy.125), channel_id=1, replica_groups=mesh['dp'=4,'ctx'=2,'seq'=4] {'seq'}, dimensions={3} | all-to-all | bytes 4718592 | tf_op jit(solution)/shard_map/all_to_all | solution.py:123
  124.3 22.6 %all-gather.12.cloned.1.call-done = bf16[4,1024,3,64]{1,3,2,0:T(8,128)(2,1)} async-done(((bf16[4,512,3,64]{1,3,2,0:T(8,128)(2,1)}), bf16[4,1024,3,64]{1,3,2,0:T(8,128)(2,1)}) %all-gather.12.cloned.1.call-update) | async-done | bytes 1572880 | tf_op jit(solution)/shard_map/all_gather | solution.py:134
  146.9 29.3 %all-gather.14.cloned.1.call-done = bf16[4,1024,3,64]{1,3,2,0:T(8,128)(2,1)} async-done(((bf16[4,512,3,64]{1,3,2,0:T(8,128)(2,1)}), bf16[4,1024,3,64]{1,3,2,0:T(8,128)(2,1)}) %all-gather.14.cloned.1.call-update) | async-done | bytes 1572880 | tf_op jit(solution)/shard_map/all_gather | solution.py:135
  176.2 45.9 %while.48 = (s32[]{:T(128)}, f32[4,512,3]{1,2,0:T(4,128)S(1)}, f32[4,512,3]{1,2,0:T(4,128)S(1)}, f32[4,512,3,64]{1,3,2,0:T(8,128)}, s32[4,1024]{1,0:T(4,128)S(1)...) while((s32[]{:T(128)}, f32[4,512,3]{1,2,0:T(4,128)S(1)}, ...), condition=%wide.region_5.6_spmd.clone, body=%wide.region_2.5_spmd.clone.sunk | while | flops 842168320 | bytes 66765076 | solution.py:30
  177.0 7.2 fusion.160
  184.2 7.7 fusion.161
  191.9 6.1 bitcast_add_fusion.9
  200.0 7.2 fusion.160
  207.2 7.6 fusion.161
  214.8 6.1 bitcast_add_fusion.9
  225.4 3.5 all-to-all-start.1
  229.1 26.9 %all-gather = bf16[8,1,384]{2,1,0:T(2,128)(2,1)S(1)} all-gather(bf16[1,1,384]{2,1,0:T(2,128)(2,1)S(1)} %reshape.191), channel_id=1, replica_groups=mesh['dp'=4,'ctx'=2,'seq'=4] {'dp','ctx'}, dimensions={0}, use_global_device_ids=true | all-gather | bytes 6912 | tf_op jit(solution)/shard_map/all_gather | solution.py:84
  259.8 39.9 %all-gather.18.cloned.1.call-done = bf16[768,3072]{1,0:T(8,128)(2,1)} async-done(((bf16[96,3072]{1,0:T(8,128)(2,1)}), bf16[768,3072]{1,0:T(8,128)(2,1)}) %all-gather.18.cloned.1.call-update) | async-done | bytes 4718608 | tf_op jit(solution)/shard_map/all_gather | solution.py:83
  299.7 7.0 fusion.82
  306.7 72.8 %all-gather.20.cloned.1.call-done = bf16[3072,768]{1,0:T(8,128)(2,1)} async-done(((bf16[384,768]{1,0:T(8,128)(2,1)}), bf16[3072,768]{1,0:T(8,128)(2,1)}) %all-gather.20.cloned.1.call-update) | async-done | bytes 4718608 | tf_op jit(solution)/shard_map/all_gather | solution.py:85
  379.5 11.1 convert_reduce_fusion
  390.5 3.5 multiply_reduce_fusion
  398.0 14.2 %all_to_all.67 = bf16[4,128,768]{1,0,2:T(4,128)(2,1)S(1)} all-to-all(bf16[4,128,768]{1,0,2:T(4,128)(2,1)S(1)} %copy.132), channel_id=1, replica_groups=mesh['dp'=4,'ctx'=2,'seq'=4] {'seq'}, dimensions={2} | all-to-all | bytes 1572864 | tf_op jit(solution)/shard_map/all_to_all | solution.py:212
  414.2 16.8 %all_gather.79 = bf16[4,1024,3]{1,2,0:T(4,128)(2,1)S(1)} all-gather(bf16[4,512,3]{1,2,0:T(4,128)(2,1)S(1)} %get-tuple-element.775), channel_id=1, replica_groups=mesh['dp'=4,'ctx'=2,'seq'=4] {'ctx'}, dimensions={1}, use_global_device_ids=true | all-gather | bytes 36864 | tf_op jit(solution)/shard_map/all_gather | solution.py:250
  436.2 33.3 %while.49 = (s32[]{:T(128)}, f32[4,512,3,64]{1,3,2,0:T(8,128)}, bf16[4,1024,3,64]{1,3,2,0:T(8,128)(2,1)S(1)}, s32[4,1024]{1,0:T(4,128)S(1)}, s32[4,512]{1,0:T(4,...) while((s32[]{:T(128)}, f32[4,512,3,64]{1,3,2,0:T(8,128)}, ...), condition=%wide.region_12.13_spmd.clone, body=%wide.region_11.12_spmd.clone.sunk | while | flops 1229062144 | bytes 34440900 | solution.py:30
  436.2 6.4 fusion.169
  443.3 9.4 bitcast_add_fusion.10
  452.8 6.4 fusion.169
  459.9 9.7 bitcast_add_fusion.10
  472.0 4.4 all_gather.81
  477.1 53.4 %while.50 = (s32[]{:T(128)}, f32[4,512,3,64]{1,3,2,0:T(8,128)}, f32[4,512,3,64]{1,3,2,0:T(8,128)}, bf16[4,1024,3,64]{1,3,2,0:T(8,128)(2,1)}, s32[4,512]{1,0:T(4,...) while((s32[]{:T(128)}, f32[4,512,3,64]{1,3,2,0:T(8,128)}, ...), condition=%wide.region_14.15_spmd.clone, body=%wide.region_13.14_spmd.clone.sunk | while | flops 1645084672 | bytes 58418928 | solution.py:30
  477.1 7.5 fusion.178
  486.1 7.9 bitcast_add_fusion.12
  494.0 9.5 bitcast_add_fusion.11
  503.5 7.5 fusion.178
  512.6 8.3 bitcast_add_fusion.12
  520.9 9.6 bitcast_add_fusion.11
  535.0 4.5 copy.135
  539.5 40.2 %all_to_all.68 = bf16[4,512,3,192]{3,0,2,1:T(4,128)(2,1)} all-to-all(bf16[4,512,3,192]{3,0,2,1:T(4,128)(2,1)S(1)} %copy.135), channel_id=1, replica_groups=mesh['dp'=4,'ctx'=2,'seq'=4] {'seq'}, dimensions={1} | all-to-all | bytes 4718592 | tf_op jit(solution)/shard_map/all_to_all | solution.py:291
  579.8 4.6 copy.137
  584.4 5.3 convolution_bitcast_fusion
  591.2 7.2 convolution_bitcast_fusion.2
  599.5 10.2 convolution_bitcast_fusion.1
  611.1 9.2 add_convert_fusion.1
  620.3 3.4 fusion.113
  625.3 91.3 %reduce-scatter.5.cloned.1.call-done = f32[96,2304]{1,0:T(8,128)} async-done(((f32[768,2304]{1,0:T(8,128)}), f32[96,2304]{1,0:T(8,128)}) %reduce-scatter.5.cloned.1.call-update) | async-done | bytes 884752 | tf_op jit(solution)/shard_map/reduce_scatter | solution.py:318
  718.6 162.9 %reduce-scatter.9.cloned.1.call-done = f32[96,3072]{1,0:T(8,128)} async-done(((f32[768,3072]{1,0:T(8,128)}), f32[96,3072]{1,0:T(8,128)}) %reduce-scatter.9.cloned.1.call-update) | async-done | bytes 1179664 | tf_op jit(solution)/shard_map/reduce_scatter | solution.py:325
  883.7 162.5 %reduce-scatter.11.cloned.1.call-done = f32[384,768]{1,0:T(8,128)} async-done(((f32[3072,768]{1,0:T(8,128)}), f32[384,768]{1,0:T(8,128)}) %reduce-scatter.11.cloned.1.call-update) | async-done | bytes 1179664 | tf_op jit(solution)/shard_map/reduce_scatter | solution.py:327
  1052.4 35.6 %all-reduce.17 = (bf16[768]{0:T(1024)(128)(2,1)S(1)}, bf16[768]{0:T(1024)(128)(2,1)S(1)}, bf16[768]{0:T(1024)(128)(2,1)S(1)}, bf16[768]{0:T(1024)(128)(2,1)S(1)}...) all-reduce(f32[768]{0:T(1024)S(1)} %get-tuple-element.672, ...), channel_id=2, replica_groups=mesh['dp'=4,'ctx'=2,'seq'=4] {'dp','ctx'}, use_global_device_ids=true, to_apply=%region_18.19.clone | all-reduce | flops 9216 | bytes 55296
  1088.7 6.4 all-reduce.19
  (286 shorter events, 79.6 us)
Async XLA Ops:
  7.2 51.4 %copy-start.4 = (bf16[4,128,768]{2,1,0:T(8,128)(2,1)S(1)}, bf16[4,128,768]{2,1,0:T(8,128)(2,1)}, u32[]{:S(2)}) copy-start(bf16[4,128,768]{2,1,0:T(8,128)(2,1)} %param.22) | copy-start | bytes 2359300
  7.2 70.8 %all-gather.10.cloned.1.call-start = ((), (), s32[]{:S(2)}) async-start(), calls=%async_computation.8 | async-start | bytes 3981312 | tf_op jit(solution)/shard_map/all_gather | solution.py:76
  7.9 139.0 %all-gather.12.cloned.1.call-start = ((), (), s32[]{:S(2)}) async-start(), calls=%async_computation.9 | async-start | bytes 2359296 | tf_op jit(solution)/shard_map/all_gather | solution.py:134
  57.2 20.8 %copy-start.28 = (f32[768]{0:T(1024)}, f32[768]{0:T(1024)S(1)}, u32[]{:S(2)}) copy-start(f32[768]{0:T(1024)S(1)} %convert_element_type.211) | copy-start | bytes 9220
  57.2 20.8 %copy-start.48 = (f32[768]{0:T(1024)}, f32[768]{0:T(1024)S(1)}, u32[]{:S(2)}) copy-start(f32[768]{0:T(1024)S(1)} %convert_element_type.212) | copy-start | bytes 9220
  58.6 19.4 %copy-start.30 = (f32[4,128]{1,0:T(4,128)}, f32[4,128]{1,0:T(4,128)S(1)}, u32[]{:S(2)}) copy-start(f32[4,128]{1,0:T(4,128)S(1)} %broadcast_multiply_fusion.1) | copy-start | bytes 6148
  59.5 18.4 %copy-start.32 = (f32[4,128]{1,0:T(4,128)}, f32[4,128]{1,0:T(4,128)S(1)}, u32[]{:S(2)}) copy-start(f32[4,128]{1,0:T(4,128)S(1)} %fusion.111) | copy-start | bytes 6148
  121.6 54.6 %all-gather.14.cloned.1.call-start = ((), (), s32[]{:S(2)}) async-start(), calls=%async_computation.10 | async-start | bytes 2359296 | tf_op jit(solution)/shard_map/all_gather | solution.py:135
  122.4 134.8 %all-gather.16.cloned.1.call-start = ((), (), s32[]{:S(2)}) async-start(), calls=%async_computation.11 | async-start | bytes 1327104 | tf_op jit(solution)/shard_map/all_gather | solution.py:79
  123.0 176.7 %all-gather.18.cloned.1.call-start = ((), (), s32[]{:S(2)}) async-start(), calls=%async_computation.12 | async-start | bytes 5308416 | tf_op jit(solution)/shard_map/all_gather | solution.py:83
  123.5 255.9 %all-gather.20.cloned.1.call-start = ((), (), s32[]{:S(2)}) async-start(), calls=%async_computation.13 | async-start | bytes 5308416 | tf_op jit(solution)/shard_map/all_gather | solution.py:85
  184.2 7.8 copy-start.14
  184.2 7.7 copy-start.59
  207.2 7.6 copy-start.14
  207.2 7.6 copy-start.59
  224.0 5.1 copy-start.56
  225.4 31.0 %all-to-all-start.1 = ((bf16[4,512,192]{2,0,1:T(4,128)(2,1)}), bf16[4,512,192]{2,0,1:T(4,128)(2,1)S(1)}, u32[]{:S(2)}, u32[]{:S(2)}) async-start(bf16[4,512,192]{2,0,1:T(4,128)(2,1)} %copy.128), calls=%async_computation.1 | async-start | bytes 2097152 | tf_op jit(solution)/shard_map/all_to_all | solution.py:159
  229.0 248.1 %all-gather.22.cloned.1.call-start = ((), (), s32[]{:S(2)}) async-start(), calls=%async_computation.14 | async-start | bytes 2359296 | tf_op jit(solution)/shard_map/all_gather | solution.py:255
  229.0 165.0 %copy-start.41 = (f32[768]{0:T(1024)}, f32[768]{0:T(1024)S(1)}, u32[]{:S(2)}) copy-start(f32[768]{0:T(1024)S(1)} %convert_element_type.219) | copy-start | bytes 9220
  229.1 70.6 %copy-start.50 = (f32[768]{0:T(1024)}, f32[768]{0:T(1024)S(1)}, u32[]{:S(2)}) copy-start(f32[768]{0:T(1024)S(1)} %convert_element_type.220) | copy-start | bytes 9220
  256.0 123.5 %copy-start.43 = (f32[8,1,384]{2,1,0:T(1,128)}, f32[8,1,384]{2,1,0:T(1,128)S(1)}, u32[]{:S(2)}) copy-start(f32[8,1,384]{2,1,0:T(1,128)S(1)} %convert_element_type.269) | copy-start | bytes 36868
  256.0 221.0 %all-gather.24.cloned.1.call-start = ((), (), s32[]{:S(2)}) async-start(), calls=%async_computation.15 | async-start | bytes 2359296 | tf_op jit(solution)/shard_map/all_gather | solution.py:256
  259.4 134.6 %copy-start.6 = (f32[4,128,768]{2,1,0:T(8,128)}, f32[4,128,768]{2,1,0:T(8,128)S(1)}, u32[]{:S(2)}) copy-start(f32[4,128,768]{2,1,0:T(8,128)S(1)} %get-tuple-element.789) | copy-start | bytes 4718596
  259.4 134.6 %copy-start.36 = (f32[4,128]{1,0:T(4,128)}, f32[4,128]{1,0:T(4,128)S(1)}, u32[]{:S(2)}) copy-start(f32[4,128]{1,0:T(4,128)S(1)} %broadcast_multiply_fusion) | copy-start | bytes 6148
  259.8 134.3 %copy-start.46 = (f32[4,128]{1,0:T(4,128)}, f32[4,128]{1,0:T(4,128)S(1)}, u32[]{:S(2)}) copy-start(f32[4,128]{1,0:T(4,128)S(1)} %fusion.112) | copy-start | bytes 6148
  259.8 119.7 %copy-start.17 = (bf16[4,128,768]{2,1,0:T(8,128)(2,1)S(1)}, bf16[4,128,768]{2,1,0:T(8,128)(2,1)}, u32[]{:S(2)}) copy-start(bf16[4,128,768]{2,1,0:T(8,128)(2,1)} %param.37) | copy-start | bytes 2359300
  379.5 11.1 copy-start.57
  390.5 3.5 copy-start.60
  412.9 18.8 %copy-start.22 = (bf16[4,128,768]{2,1,0:T(8,128)(2,1)S(1)}, bf16[4,128,768]{2,1,0:T(8,128)(2,1)}, u32[]{:S(2)}) copy-start(bf16[4,128,768]{2,1,0:T(8,128)(2,1)} %copy-done.21) | copy-start | bytes 2359300
  414.1 209.6 %reduce-scatter.7.cloned.1.call-start = ((), (), s32[]{:S(2)}) async-start(), calls=%async_computation.17 | async-start | bytes 2654208 | tf_op jit(solution)/shard_map/reduce_scatter | solution.py:321
  433.9 282.8 %reduce-scatter.5.cloned.1.call-start = ((), (), s32[]{:S(2)}) async-start(), calls=%async_computation.16 | async-start | bytes 7962624 | tf_op jit(solution)/shard_map/reduce_scatter | solution.py:318
  469.6 7.5 copy-start.3
  486.1 7.9 copy-start.10
  512.6 8.3 copy-start.10
  579.8 4.6 copy-start.5
  579.8 4.6 copy-start.29
  579.8 4.6 copy-start.31
  579.8 4.6 copy-start.33
  579.8 4.7 copy-start.49
  584.4 5.4 copy-start.11
  589.8 291.7 %reduce-scatter.9.cloned.1.call-start = ((), (), s32[]{:S(2)}) async-start(), calls=%async_computation.18 | async-start | bytes 10616832 | tf_op jit(solution)/shard_map/reduce_scatter | solution.py:325
  598.4 447.8 %reduce-scatter.11.cloned.1.call-start = ((), (), s32[]{:S(2)}) async-start(), calls=%async_computation.19 | async-start | bytes 10616832 | tf_op jit(solution)/shard_map/reduce_scatter | solution.py:327
  609.7 490.1 %all-reduce.23.cloned.1.call-start = ((), (), s32[]{:S(2)}) async-start(), calls=%async_computation.20 | async-start | bytes 3538944 | tf_op jit(solution)/shard_map/psum | solution.py:333
  611.1 9.2 copy-start.12
  611.1 9.2 copy-start.58
  620.3 3.4 copy-start.39
  883.7 164.7 %copy-start.13 = (bf16[4,128,3,4,192]{1,4,3,2,0:T(8,128)(2,1)S(1)}, bf16[4,128,3,4,192]{1,4,3,2,0:T(8,128)(2,1)}, u32[]{:S(2)}) copy-start(bf16[4,128,3,4,192]{1,4,3,2,0:T(8,128)(2,1)} %copy-done.11) | copy-start | bytes 7077892
  1099.8 3.4 copy-start.26
  (31 other events, 51.1 us)
Sparse Core Ops, SparseCore 0:
  10.2 67.7 all-gather.9
  121.8 25.0 all-gather.11
  149.0 27.1 all-gather.13
  178.3 41.1 all-gather.15
  221.5 78.1 all-gather.17
  301.7 77.6 all-gather.19
  381.6 25.5 all-gather.21
  414.2 24.9 all-gather.23
  442.7 69.5 reduce-scatter.6
  589.9 126.7 reduce-scatter.4
  720.3 161.2 reduce-scatter.8
  885.0 161.1 reduce-scatter.10
  1050.0 45.3 all-reduce.22
where the time goes:
time: 1120 us; the launch traced here: 1110 us
  waiting for transfers between devices  603 us (54%)
  blocking collectives  216 us (19%)
  matrix products  176 us (16%)
  other arithmetic  55 us (5%)
  local copies, waits for them, and re-layouts  39.5 us (4%)
  between operations  17.1 us (2%)
    reduce_scatter x1, waiting for transfers between devices, local(): lax.psum_scatter(grads[9], ('dp', 'ctx'), scatter_dimension=0, tiled=True)  163 us
    reduce_scatter x1, waiting for transfers between devices, local(): lax.psum_scatter(grads[11], ('dp', 'ctx'), scatter_dimension=0, tiled=True)  163 us
    reduce_scatter x1, waiting for transfers between devices, local(): lax.psum_scatter(grads[2], ('dp', 'ctx'), scatter_dimension=0, tiled=True)  91.3 us
    unnamed x2, blocking collectives  76.2 us
    all_gather x1, waiting for transfers between devices, local(): lax.all_gather(shards[11], ('dp', 'ctx'), axis=0, tiled=True)  72.8 us
    all_to_all x1, blocking collectives, local(): lax.all_to_all(grad_qkv_heads, 'seq', split_axis=1, concat_axis=3, tiled=...  40.2 us
    all_gather x1, waiting for transfers between devices, local(): lax.all_gather(shards[9], ('dp', 'ctx'), axis=0, tiled=True)  39.9 us
    all_to_all x1, blocking collectives, local(): lax.all_to_all(qkv_tok, 'seq', split_axis=3, concat_axis=1, tiled=True)  31 us
  transfers between devices with their start and end apart: 14, of which 8 were waited for; matrix products, arithmetic and copies ran while one was open for 22% of the time, Pallas kernels for 0%

commit v1 on v0

--- a/solution.py
+++ b/solution.py
@@ -22,6 +22,54 @@
         * up_in
         * (1.0 + jnp.tanh(0.7978845608028654 * (up_in + 0.044715 * up_in * up_in * up_in)))
     )
+
+
+def shard_count():
+    return lax.axis_size("dp") * lax.axis_size("ctx")
+
+
+def padded_length(length, multiple):
+    return -(-length // multiple) * multiple
+
+
+def gather_packed(pieces):
+    count = shard_count()
+    flat = [piece.reshape(-1) for piece in pieces]
+    length = sum(item.size for item in flat)
+    padded = padded_length(length, 1024)
+    if padded > length:
+        flat.append(jnp.zeros((padded - length,), flat[0].dtype))
+    tiles = jnp.concatenate(flat).reshape(padded // 128, 128)
+    full = lax.all_gather(tiles, ("dp", "ctx"), axis=0, tiled=True).reshape(count, padded)
+    result = []
+    offset = 0
+    for piece in pieces:
+        size = piece.size
+        part = full[:, offset : offset + size].reshape((-1,) + piece.shape[1:])
+        result.append(part)
+        offset += size
+    return result
+
+
+def reduce_packed(grads):
+    count = shard_count()
+    seq_devices = lax.axis_size("seq")
+    rows = [grad.astype(jnp.bfloat16).reshape(count, -1) for grad in grads]
+    length = sum(row.shape[1] for row in rows)
+    padded = padded_length(length, 1024 * seq_devices)
+    if padded > length:
+        rows.append(jnp.zeros((count, padded - length), jnp.bfloat16))
+    packed = jnp.concatenate(rows, axis=1).reshape(count * padded // 128, 128)
+    share = lax.psum_scatter(packed, ("dp", "ctx", "seq"), scatter_dimension=0, tiled=True)
+    total = lax.all_gather(share, "seq", axis=0, tiled=True).reshape(-1)
+    result = []
+    offset = 0
+    for grad in grads:
+        size = grad.size // count
+        shard_shape = (grad.shape[0] // count,) + grad.shape[1:]
+        result.append(total[offset : offset + size].reshape(shard_shape).astype(jnp.float32))
+        offset += size
+    return result
 
 
 def block_loop(row_count, step_fn, running):
@@ -70,21 +118,9 @@
         w_down,
         bias_down,
     )
-    whole = (
-        lax.all_gather(shards[0], ("dp", "ctx"), axis=0, tiled=True),
-        lax.all_gather(shards[1], ("dp", "ctx"), axis=0, tiled=True),
-        lax.all_gather(shards[2], ("dp", "ctx"), axis=0, tiled=True),
-        lax.all_gather(shards[3], ("dp", "ctx"), axis=0, tiled=True),
-        lax.all_gather(shards[4], ("dp", "ctx"), axis=0, tiled=True),
-        lax.all_gather(shards[5], ("dp", "ctx"), axis=0, tiled=True),
-        lax.all_gather(shards[6], ("dp", "ctx"), axis=0, tiled=True),
-        lax.all_gather(shards[7], ("dp", "ctx"), axis=0, tiled=True),
-        lax.all_gather(shards[8], ("dp", "ctx"), axis=0, tiled=True),
-        lax.all_gather(shards[9], ("dp", "ctx"), axis=0, tiled=True),
-        lax.all_gather(shards[10], ("dp", "ctx"), axis=0, tiled=True),
-        lax.all_gather(shards[11], ("dp", "ctx"), axis=0, tiled=True),
-        lax.all_gather(shards[12], ("dp", "ctx"), axis=0, tiled=True),
-    )
+    gathered_a = gather_packed(shards[:9])
+    gathered_m = gather_packed(shards[9:])
+    whole = tuple(gathered_a) + tuple(gathered_m)
     (
         whole_attn_gain,
         whole_attn_shift,
@@ -174,25 +210,10 @@
         + jnp.dot(active_b, whole_w_down, preferred_element_type=f32)
         + whole_bias_down.astype(f32)
     ).astype(bf16)
-    again = (
-        lax.all_gather(shards[0], ("dp", "ctx"), axis=0, tiled=True),
-        lax.all_gather(shards[1], ("dp", "ctx"), axis=0, tiled=True),
-        lax.all_gather(shards[2], ("dp", "ctx"), axis=0, tiled=True),
-        lax.all_gather(shards[3], ("dp", "ctx"), axis=0, tiled=True),
-        lax.all_gather(shards[4], ("dp", "ctx"), axis=0, tiled=True),
-        lax.all_gather(shards[5], ("dp", "ctx"), axis=0, tiled=True),
-        lax.all_gather(shards[6], ("dp", "ctx"), axis=0, tiled=True),
-        lax.all_gather(shards[7], ("dp", "ctx"), axis=0, tiled=True),
-        lax.all_gather(shards[8], ("dp", "ctx"), axis=0, tiled=True),
-        lax.all_gather(shards[9], ("dp", "ctx"), axis=0, tiled=True),
-        lax.all_gather(shards[10], ("dp", "ctx"), axis=0, tiled=True),
-        lax.all_gather(shards[11], ("dp", "ctx"), axis=0, tiled=True),
-        lax.all_gather(shards[12], ("dp", "ctx"), axis=0, tiled=True),
-    )
-    back_w_qkv = again[2]
-    back_w_out = again[5]
-    back_w_up = again[9]
-    back_w_down = again[11]
+    back_w_qkv = whole_w_qkv
+    back_w_out = whole_w_out
+    back_w_up = whole_w_up
+    back_w_down = whole_w_down
     grad_w_down = jnp.einsum("nsf,nsd->fd", active_b, cotangent, preferred_element_type=f32)
     grad_bias_down = jnp.sum(cotangent, axis=(0, 1), dtype=f32)
     grad_active = jnp.einsum("nsd,fd->nsf", cotangent, back_w_down, preferred_element_type=f32)
@@ -297,52 +318,22 @@
     grad_normed_a = jnp.einsum("nsc,dc->nsd", grad_qkv, back_w_qkv, preferred_element_type=f32)
     grad_input_norm, grad_attn_gain, grad_attn_shift = pull_attn(grad_normed_a)
     grad_input = (grad_hidden + grad_input_norm).astype(bf16)
-    grads = (
-        grad_attn_gain,
-        grad_attn_shift,
-        grad_w_qkv,
-        grad_bias_query,
-        grad_bias_value,
-        grad_w_out,
-        grad_bias_out,
-        grad_mlp_gain,
-        grad_mlp_shift,
-        grad_w_up,
-        grad_bias_up,
-        grad_w_down,
-        grad_bias_down,
-    )
-    shares = (
-        lax.psum_scatter(grads[0], ("dp", "ctx"), scatter_dimension=0, tiled=True),
-        lax.psum_scatter(grads[1], ("dp", "ctx"), scatter_dimension=0, tiled=True),
-        lax.psum_scatter(grads[2], ("dp", "ctx"), scatter_dimension=0, tiled=True),
-        lax.psum_scatter(grads[3], ("dp", "ctx"), scatter_dimension=0, tiled=True),
-        lax.psum_scatter(grads[4], ("dp", "ctx"), scatter_dimension=0, tiled=True),
-        lax.psum_scatter(grads[5], ("dp", "ctx"), scatter_dimension=0, tiled=True),
-        lax.psum_scatter(grads[6], ("dp", "ctx"), scatter_dimension=0, tiled=True),
-        lax.psum_scatter(grads[7], ("dp", "ctx"), scatter_dimension=0, tiled=True),
-        lax.psum_scatter(grads[8], ("dp", "ctx"), scatter_dimension=0, tiled=True),
-        lax.psum_scatter(grads[9], ("dp", "ctx"), scatter_dimension=0, tiled=True),
-        lax.psum_scatter(grads[10], ("dp", "ctx"), scatter_dimension=0, tiled=True),
-        lax.psum_scatter(grads[11], ("dp", "ctx"), scatter_dimension=0, tiled=True),
-        lax.psum_scatter(grads[12], ("dp", "ctx"), scatter_dimension=0, tiled=True),
-    )
-    totals = (
-        lax.psum(shares[0].astype(jnp.bfloat16), "seq").astype(jnp.float32),
-        lax.psum(shares[1].astype(jnp.bfloat16), "seq").astype(jnp.float32),
-        lax.psum(shares[2].astype(jnp.bfloat16), "seq").astype(jnp.float32),
-        lax.psum(shares[3].astype(jnp.bfloat16), "seq").astype(jnp.float32),
-        lax.psum(shares[4].astype(jnp.bfloat16), "seq").astype(jnp.float32),
-        lax.psum(shares[5].astype(jnp.bfloat16), "seq").astype(jnp.float32),
-        lax.psum(shares[6].astype(jnp.bfloat16), "seq").astype(jnp.float32),
-        lax.psum(shares[7].astype(jnp.bfloat16), "seq").astype(jnp.float32),
-        lax.psum(shares[8].astype(jnp.bfloat16), "seq").astype(jnp.float32),
-        lax.psum(shares[9].astype(jnp.bfloat16), "seq").astype(jnp.float32),
-        lax.psum(shares[10].astype(jnp.bfloat16), "seq").astype(jnp.float32),
-        lax.psum(shares[11].astype(jnp.bfloat16), "seq").astype(jnp.float32),
-        lax.psum(shares[12].astype(jnp.bfloat16), "seq").astype(jnp.float32),
-    )
-    return (layer_output, grad_input) + tuple(totals)
+    mlp_totals = reduce_packed(
+        (
+            grad_w_out,
+            grad_bias_out,
+            grad_mlp_gain,
+            grad_mlp_shift,
+            grad_w_up,
+            grad_bias_up,
+            grad_w_down,
+            grad_bias_down,
+        )
+    )
+    attn_totals = reduce_packed(
+        (grad_attn_gain, grad_attn_shift, grad_w_qkv, grad_bias_query, grad_bias_value)
+    )
+    return (layer_output, grad_input) + tuple(attn_totals) + tuple(mlp_totals)
 
 
 def solution(mesh):

time: 1120 us -> 1010 us (0.902)
  local copies, waits for them, and re-layouts: 39.5 us -> 260 us
  blocking collectives: 216 us -> 46.4 us
  waiting for transfers between devices: 603 us -> 440 us
    reduce_scatter x4 -> x0, waiting for transfers between devices: 417 us -> none  [the longest x1 163 us: local(): lax.psum_scatter(grads[9], ('dp', 'ctx'), scatter_dimension=0, tiled=True)]
    unnamed x13 -> x11, waiting for transfers between devices: 2.86 us -> 224 us
    reshape x0 -> x20, local copies, waits for them, and re-layouts: none -> 85.2 us  [the longest x9 24.6 us: reduce_packed(): rows = [grad.astype(jnp.bfloat16).reshape(count, -1) for grad in grads]]
    unnamed x2 -> x0, blocking collectives: 76.2 us -> none
    unnamed x143 -> x139, local copies, waits for them, and re-layouts: 14.9 us -> 87.7 us
    all_to_all x2 -> x0, blocking collectives: 54.4 us -> none  [the longest x1 40.2 us: local(): lax.all_to_all(grad_qkv_heads, 'seq', split_axis=1, concat_axis=3, tiled=...]
    concatenate x0 -> x6, local copies, waits for them, and re-layouts: none -> 32.4 us  [the longest x2 31 us: gather_packed(): tiles = jnp.concatenate(flat).reshape(padded // 128, 128)]
    all_gather x4 -> x3, waiting for transfers between devices: 131 us -> 162 us  [the longest x2 147 us: gather_packed(): lax.all_gather(tiles, ('dp', 'ctx'), axis=0, tiled=True)]
  transfers between devices with their start and end apart: 14 -> 12, of which waited for: 8 -> 10; matrix products, arithmetic and copies ran while one was open for 22% -> 29% of each run, Pallas kernels for 0% -> 0%
where the time goes in v1:
time: 1010 us; the launch traced here: 993 us
  waiting for transfers between devices  440 us (44%)
  local copies, waits for them, and re-layouts  260 us (26%)
  matrix products  171 us (17%)
  blocking collectives  46.4 us (5%)
  other arithmetic  46.1 us (5%)
  between operations  15.2 us (2%)
  starting transfers between devices  13.4 us (1%)
    unnamed x11, waiting for transfers between devices  224 us
    all_gather x2, waiting for transfers between devices, gather_packed(): lax.all_gather(tiles, ('dp', 'ctx'), axis=0, tiled=True)  147 us
    unnamed x139, local copies, waits for them, and re-layouts  87.7 us
    all_to_all x1, blocking collectives, local(): lax.all_to_all(qkv_tok, 'seq', split_axis=3, concat_axis=1, tiled=True)  31 us
    concatenate x2, local copies, waits for them, and re-layouts, gather_packed(): tiles = jnp.concatenate(flat).reshape(padded // 128, 128)  31 us
    all_gather x1, waiting for transfers between devices, local(): value_piece = lax.all_gather(value_rows, 'ctx', axis=1, tiled=True)  29.3 us
    dot_general x4, matrix products, query_grads(): jnp.einsum('nqhd,nkhd->nqhk', query_block, key_block, preferred_element_t...  28.5 us
    reshape x9, local copies, waits for them, and re-layouts, reduce_packed(): rows = [grad.astype(jnp.bfloat16).reshape(count, -1) for grad in grads]  24.6 us
  transfers between devices with their start and end apart: 12, of which 10 were waited for; matrix products, arithmetic and copies ran while one was open for 29% of the time, Pallas kernels for 0%

profile of v1, /device:TPU:0, one launch (start us, length us, event | category | flops | bytes accessed | tf_op | source)
XLA Modules:
  0.0 993.3 jit_solution(10579399754679995529)
XLA Ops:
  9.9 17.2 %concatenate.23 = bf16[295936]{0:T(1024)(128)(2,1)} concatenate(bf16[96]{0:T(256)(128)(2,1)} %param.24, bf16[96]{0:T(256)(128)(2,1)} %param.25, bf16[221184]{0:T(1024)(128)(2,1)S(1)} %reshape.318, bf16[96]{0:T(256)(128)(2,1)} %param.27, bf16[96]{0:T(256)(128)(2,1)} %param.28, bf16[73728]{0:T(1024)(128)(2,1)S(1)} %reshape.319, bf16[96]{0:T(256)(128)(2,1)} %param.30, ...), dimensions={0} | concatenate | bytes 1183744 | tf_op jit(solution)/shard_map/concatenate | solution.py:42
  27.8 81.8 %all-gather.8.cloned.1.call-done = bf16[18496,128]{1,0:T(8,128)(2,1)} async-done(((bf16[2312,128]{1,0:T(8,128)(2,1)}), bf16[18496,128]{1,0:T(8,128)(2,1)}) %all-gather.8.cloned.1.call-update) | async-done | bytes 4734992 | tf_op jit(solution)/shard_map/all_gather | solution.py:43
  109.5 6.4 reshape.321
  139.7 31.0 %all_to_all.66 = bf16[4,128,3,768]{1,0,2,3:T(4,128)(2,1)S(1)} all-to-all(bf16[4,128,3,768]{1,0,2,3:T(4,128)(2,1)S(1)} %copy.125), channel_id=1, replica_groups=mesh['dp'=4,'ctx'=2,'seq'=4] {'seq'}, dimensions={3} | all-to-all | bytes 4718592 | tf_op jit(solution)/shard_map/all_to_all | solution.py:159
  175.9 13.8 %concatenate.27 = bf16[590848]{0:T(1024)(128)(2,1)} concatenate(bf16[294912]{0:T(1024)(128)(2,1)S(1)} %bitcast.211, bf16[384]{0:T(512)(128)(2,1)S(1)} %copy-done.60, bf16[294912]{0:T(1024)(128)(2,1)S(1)} %reshape.326, bf16[96]{0:T(256)(128)(2,1)S(1)} %copy-done.61, bf16[544]{0:T(1024)(128)(2,1)S(1)} %broadcast_in_dim.170), dimensions={0} | concatenate | bytes 2363392 | tf_op jit(solution)/shard_map/concatenate | solution.py:42
  189.9 7.7 all-gather.10.cloned.1.call-done
  197.7 29.3 %all-gather.12.cloned.1.call-done = bf16[4,1024,3,64]{1,3,2,0:T(8,128)(2,1)} async-done(((bf16[4,512,3,64]{1,3,2,0:T(8,128)(2,1)}), bf16[4,1024,3,64]{1,3,2,0:T(8,128)(2,1)}) %all-gather.12.cloned.1.call-update) | async-done | bytes 1572880 | tf_op jit(solution)/shard_map/all_gather | solution.py:171
  227.0 47.1 %while.48 = (s32[]{:T(128)}, f32[4,512,3]{1,2,0:T(4,128)S(1)}, f32[4,512,3]{1,2,0:T(4,128)S(1)}, f32[4,512,3,64]{1,3,2,0:T(8,128)}, s32[4,1024]{1,0:T(4,128)S(1)...) while((s32[]{:T(128)}, f32[4,512,3]{1,2,0:T(4,128)S(1)}, ...), condition=%wide.region_5.6_spmd.clone, body=%wide.region_2.5_spmd.clone.sunk | while | flops 842168320 | bytes 66765084 | solution.py:78
  227.8 7.2 fusion.157
  235.0 8.7 fusion.158
  243.8 6.2 bitcast_add_fusion.9
  251.8 7.2 fusion.157
  259.1 7.6 fusion.158
  266.8 6.1 bitcast_add_fusion.9
  284.6 11.5 %all-to-all-done.1 = bf16[4,512,192]{2,0,1:T(4,128)(2,1)} async-done(((bf16[4,512,192]{2,0,1:T(4,128)(2,1)}), bf16[4,512,192]{2,0,1:T(4,128)(2,1)}, u32[]{:S(2)}, u32[]{:S(2)}) %all-to-all-start.1) | async-done | bytes 786464 | tf_op jit(solution)/shard_map/all_to_all | solution.py:195
  300.8 65.7 %all-gather.14.cloned.1.call-done = bf16[36928,128]{1,0:T(8,128)(2,1)} async-done(((bf16[4616,128]{1,0:T(8,128)(2,1)}), bf16[36928,128]{1,0:T(8,128)(2,1)}) %all-gather.14.cloned.1.call-update) | async-done | bytes 9453584 | tf_op jit(solution)/shard_map/all_gather | solution.py:43
  366.5 11.3 %reshape.328 = bf16[8,590848]{1,0:T(8,128)(2,1)} reshape(bf16[36928,128]{1,0:T(8,128)(2,1)} %all-gather.14.cloned.1.call-done) | data formatting | bytes 18907136 | tf_op jit(solution)/shard_map/reshape | solution.py:43
  377.8 8.3 fusion.105
  386.8 6.6 reshape.360
  393.5 6.6 reshape.359
  405.1 8.4 fusion.108
  432.1 5.8 all-to-all-done.2
  443.4 33.8 %while.49 = (s32[]{:T(128)}, f32[4,512,3,64]{1,3,2,0:T(8,128)}, bf16[4,1024,3,64]{1,3,2,0:T(8,128)(2,1)S(1)}, s32[4,1024]{1,0:T(4,128)S(1)}, s32[4,512]{1,0:T(4,...) while((s32[]{:T(128)}, f32[4,512,3,64]{1,3,2,0:T(8,128)}, ...), condition=%wide.region_12.13_spmd.clone, body=%wide.region_11.12_spmd.clone.sunk | while | flops 1229062144 | bytes 34539240 | solution.py:78
  443.4 6.8 fusion.166
  451.0 9.4 bitcast_add_fusion.10
  460.4 6.4 fusion.166
  467.6 9.6 bitcast_add_fusion.10
  484.8 53.8 %while.50 = (s32[]{:T(128)}, f32[4,512,3,64]{1,3,2,0:T(8,128)}, f32[4,512,3,64]{1,3,2,0:T(8,128)}, bf16[4,1024,3,64]{1,3,2,0:T(8,128)(2,1)}, s32[4,512]{1,0:T(4,...) while((s32[]{:T(128)}, f32[4,512,3,64]{1,3,2,0:T(8,128)}, ...), condition=%wide.region_14.15_spmd.clone, body=%wide.region_13.14_spmd.clone.sunk | while | flops 1645084672 | bytes 58418936 | solution.py:78
  485.2 7.7 fusion.175
  494.4 9.4 bitcast_add_fusion.11
  503.9 7.7 bitcast_add_fusion.12
  511.6 7.6 fusion.175
  520.8 9.6 bitcast_add_fusion.11
  530.4 8.2 bitcast_add_fusion.12
  556.6 6.7 bitcast_convert_fusion.1
  563.3 6.7 reshape.340
  570.0 8.8 bitcast_convert_fusion
  578.8 6.6 reshape.342
  586.4 6.0 copy.137
  618.3 19.5 %dynamic-update-slice.11 = bf16[8,225280]{1,0:T(8,128)(2,1)} dynamic-update-slice(bf16[8,225280]{1,0:T(8,128)(2,1)} %dynamic-update-slice.10, bf16[8,221184]{1,0:T(8,128)(2,1)} %reshape.333, s32[]{} %constant.193, s32[]{} %constant.203) | dynamic-update-slice | bytes 7077892
  652.5 25.7 %dynamic-update-slice.4 = bf16[8,667648]{1,0:T(8,128)(2,1)} dynamic-update-slice(bf16[8,667648]{1,0:T(8,128)(2,1)} %dynamic-update-slice.3, bf16[8,294912]{1,0:T(8,128)(2,1)} %reshape.340, s32[]{} %constant.193, s32[]{} %constant.197) | dynamic-update-slice | bytes 9437188
  679.6 25.5 %dynamic-update-slice.6 = bf16[8,667648]{1,0:T(8,128)(2,1)} dynamic-update-slice(bf16[8,667648]{1,0:T(8,128)(2,1)} %dynamic-update-slice.5, bf16[8,294912]{1,0:T(8,128)(2,1)} %reshape.342, s32[]{} %constant.193, s32[]{} %constant.199) | dynamic-update-slice | bytes 9437188
  707.2 12.9 %reshape.344 = bf16[41728,128]{1,0:T(8,128)(2,1)} reshape(bf16[8,667648]{1,0:T(8,128)(2,1)} %broadcast_dynamic-update-slice_fusion.1) | data formatting | bytes 21364736 | tf_op jit(solution)/shard_map/reshape | solution.py:62
  721.0 9.2 add_convert_fusion.1
  731.9 60.5 %reduce-scatter.9.cloned.1.call-done = bf16[440,128]{1,0:T(8,128)(2,1)} async-done(((bf16[14080,128]{1,0:T(8,128)(2,1)}), bf16[440,128]{1,0:T(8,128)(2,1)}) %reduce-scatter.9.cloned.1.call-update) | async-done | bytes 112656
  792.4 6.5 all_gather.40
  798.9 162.3 %reduce-scatter.11.cloned.1.call-done = bf16[1304,128]{1,0:T(8,128)(2,1)} async-done(((bf16[41728,128]{1,0:T(8,128)(2,1)}), bf16[1304,128]{1,0:T(8,128)(2,1)}) %reduce-scatter.11.cloned.1.call-update) | async-done | bytes 333840
  963.2 14.5 %all-gather.20.cloned.1.call-done = bf16[5216,128]{1,0:T(8,128)(2,1)} async-done(((bf16[1304,128]{1,0:T(8,128)(2,1)}), bf16[5216,128]{1,0:T(8,128)(2,1)}) %all-gather.20.cloned.1.call-update) | async-done | bytes 1335312 | tf_op jit(solution)/shard_map/all_gather | solution.py:64
  (308 shorter events, 168.9 us)
Async XLA Ops:
  7.2 20.0 %copy-start.4 = (bf16[4,128,768]{2,1,0:T(8,128)(2,1)S(1)}, bf16[4,128,768]{2,1,0:T(8,128)(2,1)}, u32[]{:S(2)}) copy-start(bf16[4,128,768]{2,1,0:T(8,128)(2,1)} %param.22) | copy-start | bytes 2359300
  7.2 102.3 %all-gather.8.cloned.1.call-start = ((), (), s32[]{:S(2)}) async-start(), calls=%async_computation.6 | async-start | bytes 5326848 | tf_op jit(solution)/shard_map/all_gather | solution.py:43
  27.1 170.6 %all-gather.10.cloned.1.call-start = ((), (), s32[]{:S(2)}) async-start(), calls=%async_computation.7 | async-start | bytes 2359296 | tf_op jit(solution)/shard_map/all_gather | solution.py:170
  27.3 99.0 %copy-start.32 = (f32[4,128]{1,0:T(4,128)}, f32[4,128]{1,0:T(4,128)S(1)}, u32[]{:S(2)}) copy-start(f32[4,128]{1,0:T(4,128)S(1)} %broadcast_multiply_fusion.1) | copy-start | bytes 6148
  27.7 88.2 %copy-start.36 = (f32[4,128]{1,0:T(4,128)}, f32[4,128]{1,0:T(4,128)S(1)}, u32[]{:S(2)}) copy-start(f32[4,128]{1,0:T(4,128)S(1)} %fusion.89) | copy-start | bytes 6148
  27.7 98.6 %copy-start.40 = (f32[4,128]{1,0:T(4,128)}, f32[4,128]{1,0:T(4,128)S(1)}, u32[]{:S(2)}) copy-start(f32[4,128]{1,0:T(4,128)S(1)} %fusion.98) | copy-start | bytes 6148
  172.9 54.1 %all-gather.12.cloned.1.call-start = ((), (), s32[]{:S(2)}) async-start(), calls=%async_computation.8 | async-start | bytes 2359296 | tf_op jit(solution)/shard_map/all_gather | solution.py:171
  173.6 192.9 %all-gather.14.cloned.1.call-start = ((), (), s32[]{:S(2)}) async-start(), calls=%async_computation.9 | async-start | bytes 10635264 | tf_op jit(solution)/shard_map/all_gather | solution.py:43
  174.2 15.6 %copy-start.59 = (s32[4,8]{1,0:T(4,128)S(1)}, s32[4,8]{1,0:T(4,128)}, u32[]{:S(2)}) copy-start(s32[4,8]{1,0:T(4,128)} %param.23) | copy-start | bytes 388
  235.0 8.8 copy-start.13
  235.0 8.8 copy-start.62
  259.1 7.7 copy-start.13
  259.1 7.7 copy-start.62
  277.4 18.8 %all-to-all-start.1 = ((bf16[4,512,192]{2,0,1:T(4,128)(2,1)}), bf16[4,512,192]{2,0,1:T(4,128)(2,1)}, u32[]{:S(2)}, u32[]{:S(2)}) async-start(bf16[4,512,192]{2,0,1:T(4,128)(2,1)} %copy.128), calls=%async_computation.1 | async-start | bytes 2097152 | tf_op jit(solution)/shard_map/all_to_all | solution.py:195
  281.7 203.1 %all-gather.16.cloned.1.call-start = ((), (), s32[]{:S(2)}) async-start(), calls=%async_computation.10 | async-start | bytes 2359296 | tf_op jit(solution)/shard_map/all_gather | solution.py:276
  284.5 115.6 %copy-start.58 = (f32[768]{0:T(1024)}, f32[768]{0:T(1024)S(1)}, u32[]{:S(2)}) copy-start(f32[768]{0:T(1024)S(1)} %reshape.350) | copy-start | bytes 9220
  284.6 132.4 %copy-start.45 = (f32[768]{0:T(1024)}, f32[768]{0:T(1024)S(1)}, u32[]{:S(2)}) copy-start(f32[768]{0:T(1024)S(1)} %reshape.349) | copy-start | bytes 9220
  300.5 116.5 %copy-start.6 = (f32[4,128,768]{2,1,0:T(8,128)}, f32[4,128,768]{2,1,0:T(8,128)S(1)}, u32[]{:S(2)}) copy-start(f32[4,128,768]{2,1,0:T(8,128)S(1)} %get-tuple-element.775) | copy-start | bytes 4718596
  300.5 116.5 %copy-start.34 = (f32[4,128]{1,0:T(4,128)}, f32[4,128]{1,0:T(4,128)S(1)}, u32[]{:S(2)}) copy-start(f32[4,128]{1,0:T(4,128)S(1)} %broadcast_multiply_fusion) | copy-start | bytes 6148
  300.8 116.2 %copy-start.49 = (f32[4,128]{1,0:T(4,128)}, f32[4,128]{1,0:T(4,128)S(1)}, u32[]{:S(2)}) copy-start(f32[4,128]{1,0:T(4,128)S(1)} %fusion.99) | copy-start | bytes 6148
  400.1 13.3 %slice-start.1 = ((s8[4718592]{0:T(1024)(128)(4,1)}), s8[4194304]{0:T(1024)(128)(4,1)S(1)}, s32[]{:S(2)}) async-start(s8[4718592]{0:T(1024)(128)(4,1)} %bitcast.199), calls=%async_computation.16 | async-start | bytes 8388608
  405.0 8.4 copy-start.63
  405.0 8.4 slice-start.2
  422.8 15.1 %all-to-all-start.2 = ((bf16[4,128,768]{1,0,2:T(4,128)(2,1)}), bf16[4,128,768]{1,0,2:T(4,128)(2,1)S(1)}, u32[]{:S(2)}, u32[]{:S(2)}) async-start(bf16[4,128,768]{1,0,2:T(4,128)(2,1)} %copy.132), calls=%async_computation.2 | async-start | bytes 1572864 | tf_op jit(solution)/shard_map/all_to_all | solution.py:233
  426.3 58.5 %all-gather.18.cloned.1.call-start = ((), (), s32[]{:S(2)}) async-start(), calls=%async_computation.11 | async-start | bytes 2359296 | tf_op jit(solution)/shard_map/all_gather | solution.py:277
  443.4 7.6 copy-start.31
  460.4 7.1 copy-start.31
  477.2 7.6 copy-start.3
  485.2 9.2 copy-start.10
  511.6 9.2 copy-start.10
  544.6 41.8 %all-to-all-start.3 = ((bf16[4,512,3,192]{3,0,2,1:T(4,128)(2,1)}), bf16[4,512,3,192]{3,0,2,1:T(4,128)(2,1)}, u32[]{:S(2)}, u32[]{:S(2)}) async-start(bf16[4,512,3,192]{3,0,2,1:T(4,128)(2,1)} %copy.135), calls=%async_computation.3 | async-start | bytes 6291456 | tf_op jit(solution)/shard_map/all_to_all | solution.py:312
  549.4 7.1 copy-start.7
  549.4 7.1 copy-start.35
  549.5 7.1 copy-start.46
  549.5 7.1 copy-start.50
  549.5 242.9 %reduce-scatter.9.cloned.1.call-start = ((), (), s32[]{:S(2)}) async-start(), calls=%async_computation.13 | async-start | bytes 3717120
  563.3 6.7 copy-start.55
  563.3 6.7 copy-start.23
  646.8 314.4 %reduce-scatter.11.cloned.1.call-start = ((), (), s32[]{:S(2)}) async-start(), calls=%async_computation.14 | async-start | bytes 11016192
  679.6 25.5 %copy-start.51 = (bf16[8,96]{1,0:T(8,128)(2,1)S(1)}, bf16[8,96]{1,0:T(8,128)(2,1)}, u32[]{:S(2)}) copy-start(bf16[8,96]{1,0:T(8,128)(2,1)} %reshape.343) | copy-start | bytes 4612
  720.2 257.5 %all-gather.20.cloned.1.call-start = ((), (), s32[]{:S(2)}) async-start(), calls=%async_computation.12 | async-start | bytes 1669120 | tf_op jit(solution)/shard_map/all_gather | solution.py:64
  721.0 9.3 copy-start.54
  721.0 9.3 copy-start.9
  721.0 9.3 copy-start.16
  721.0 9.3 copy-start.24
  721.0 9.3 copy-start.39
  721.0 9.3 copy-start.42
  721.0 9.3 copy-start.44
  (37 other events, 138.6 us)
Sparse Core Ops, SparseCore 0:
  27.2 82.2 all-gather.7
  173.0 24.6 all-gather.9
  199.8 27.1 all-gather.11
  229.1 137.4 all-gather.13
  368.5 25.3 all-gather.15
  443.5 24.6 all-gather.17
  647.0 145.4 reduce-scatter.8
  794.7 166.4 reduce-scatter.10
  962.8 14.8 all-gather.19

commit v2 on v1

--- a/solution.py
+++ b/solution.py
@@ -70,6 +70,13 @@
         result.append(total[offset : offset + size].reshape(shard_shape).astype(jnp.float32))
         offset += size
     return result
+
+
+def reduce_matrix(grad):
+    share = lax.psum_scatter(
+        grad.astype(jnp.bfloat16), ("dp", "ctx", "seq"), scatter_dimension=0, tiled=True
+    )
+    return lax.all_gather(share, "seq", axis=0, tiled=True).astype(jnp.float32)
 
 
 def block_loop(row_count, step_fn, running):
@@ -118,9 +125,13 @@
         w_down,
         bias_down,
     )
-    gathered_a = gather_packed(shards[:9])
-    gathered_m = gather_packed(shards[9:])
-    whole = tuple(gathered_a) + tuple(gathered_m)
+    vector_ids = (0, 1, 3, 4, 6, 7, 8, 10, 12)
+    vectors = gather_packed(tuple(shards[index] for index in vector_ids))
+    whole = [None] * len(shards)
+    for index, value in zip(vector_ids, vectors):
+        whole[index] = value
+    for index in (2, 5, 9, 11):
+        whole[index] = lax.all_gather(shards[index], ("dp", "ctx"), axis=0, tiled=True)
     (
         whole_attn_gain,
         whole_attn_shift,
@@ -230,6 +241,14 @@
     grad_context = jnp.einsum(
         "nsd,cd->nsc", grad_att, back_w_out, preferred_element_type=f32
     ).astype(bf16)
+    grad_w_down, grad_w_up, grad_w_out, grad_context = lax.optimization_barrier(
+        (grad_w_down, grad_w_up, grad_w_out, grad_context)
+    )
+    mlp_totals = {
+        11: reduce_matrix(grad_w_down),
+        9: reduce_matrix(grad_w_up),
+        5: reduce_matrix(grad_w_out),
+    }
     grad_out_h = lax.all_to_all(
         grad_context, "seq", split_axis=2, concat_axis=1, tiled=True
     ).reshape(head_shape)
@@ -318,22 +337,29 @@
     grad_normed_a = jnp.einsum("nsc,dc->nsd", grad_qkv, back_w_qkv, preferred_element_type=f32)
     grad_input_norm, grad_attn_gain, grad_attn_shift = pull_attn(grad_normed_a)
     grad_input = (grad_hidden + grad_input_norm).astype(bf16)
-    mlp_totals = reduce_packed(
-        (
-            grad_w_out,
-            grad_bias_out,
-            grad_mlp_gain,
-            grad_mlp_shift,
-            grad_w_up,
-            grad_bias_up,
-            grad_w_down,
-            grad_bias_down,
-        )
-    )
-    attn_totals = reduce_packed(
-        (grad_attn_gain, grad_attn_shift, grad_w_qkv, grad_bias_query, grad_bias_value)
-    )
-    return (layer_output, grad_input) + tuple(attn_totals) + tuple(mlp_totals)
+    grads = [
+        grad_attn_gain,
+        grad_attn_shift,
+        grad_w_qkv,
+        grad_bias_query,
+        grad_bias_value,
+        grad_w_out,
+        grad_bias_out,
+        grad_mlp_gain,
+        grad_mlp_shift,
+        grad_w_up,
+        grad_bias_up,
+        grad_w_down,
+        grad_bias_down,
+    ]
+    totals = [None] * len(grads)
+    vector_totals = reduce_packed(tuple(grads[index] for index in vector_ids))
+    for index, value in zip(vector_ids, vector_totals):
+        totals[index] = value
+    for index in (11, 9, 5):
+        totals[index] = mlp_totals[index]
+    totals[2] = reduce_matrix(grads[2])
+    return (layer_output, grad_input) + tuple(totals)
 
 
 def solution(mesh):

time: 1010 us -> 1120 us (1.11)
  waiting for transfers between devices: 440 us -> 719 us
  local copies, waits for them, and re-layouts: 260 us -> 39.4 us
  blocking collectives: 46.4 us -> 107 us
    reduce_scatter x0 -> x4, waiting for transfers between devices: none -> 343 us  [reduce_matrix(): lax.psum_scatter(grad.astype(jnp.bfloat16), ('dp', 'ctx', 'seq'), scatter...]
    unnamed x11 -> x14, waiting for transfers between devices: 224 us -> 119 us
    unnamed x139 -> x82, local copies, waits for them, and re-layouts: 87.7 us -> 8.65 us
    all_gather x0 -> x5, blocking collectives: none -> 61 us  [the longest x1 33 us: gather_packed(): lax.all_gather(tiles, ('dp', 'ctx'), axis=0, tiled=True)]
    all_to_all x1, waiting for transfers between devices: 0.26 us -> 35.7 us  [local(): lax.all_to_all(grad_qkv_heads, 'seq', split_axis=1, concat_axis=3, tiled=...]
    concatenate x2 -> x1, local copies, waits for them, and re-layouts: 31 us -> 6.12 us  [gather_packed(): tiles = jnp.concatenate(flat).reshape(padded // 128, 128)]
    reshape x7 -> x0, local copies, waits for them, and re-layouts: 24.5 us -> none  [the longest x4 20.2 us: gather_packed(): part = full[:, offset:offset + size].reshape((-1,) + piece.shape[1:])]
    reshape x9 -> x5, local copies, waits for them, and re-layouts: 24.6 us -> 0.35 us  [reduce_packed(): rows = [grad.astype(jnp.bfloat16).reshape(count, -1) for grad in grads]]
  transfers between devices with their start and end apart: 12 -> 16, of which waited for: 10 -> 13; matrix products, arithmetic and copies ran while one was open for 29% -> 16% of each run, Pallas kernels for 0% -> 0%
where the time goes in v2:
time: 1120 us; the launch traced here: 1110 us
  waiting for transfers between devices  719 us (64%)
  matrix products  173 us (15%)
  blocking collectives  107 us (10%)
  other arithmetic  44.5 us (4%)
  local copies, waits for them, and re-layouts  39.4 us (4%)
  between operations  15 us (1%)
  starting transfers between devices  12.2 us (1%)
    reduce_scatter x4, waiting for transfers between devices, reduce_matrix(): lax.psum_scatter(grad.astype(jnp.bfloat16), ('dp', 'ctx', 'seq'), scatter...  343 us
    all_gather x4, waiting for transfers between devices, local(): lax.all_gather(shards[index], ('dp', 'ctx'), axis=0, tiled=True)  149 us
    unnamed x14, waiting for transfers between devices  119 us
    all_to_all x1, waiting for transfers between devices, local(): lax.all_to_all(grad_qkv_heads, 'seq', split_axis=1, concat_axis=3, tiled=...  35.7 us
    all_gather x1, blocking collectives, gather_packed(): lax.all_gather(tiles, ('dp', 'ctx'), axis=0, tiled=True)  33 us
    all_to_all x1, blocking collectives, local(): lax.all_to_all(qkv_tok, 'seq', split_axis=3, concat_axis=1, tiled=True)  31 us
    all_gather x1, waiting for transfers between devices, local(): key_piece = lax.all_gather(key_rows, 'ctx', axis=1, tiled=True)  29.3 us
    dot_general x4, matrix products, query_grads(): jnp.einsum('nqhd,nkhd->nqhk', query_block, key_block, preferred_element_t...  28.2 us
  transfers between devices with their start and end apart: 16, of which 13 were waited for; matrix products, arithmetic and copies ran while one was open for 16% of the time, Pallas kernels for 0%

profile of v2, /device:TPU:0, one launch (start us, length us, event | category | flops | bytes accessed | tf_op | source)
XLA Modules:
  0.0 1109.8 jit_solution(5620014001809216826)
XLA Ops:
  8.0 6.1 concatenate.17
  14.1 33.0 %all_gather.50 = bf16[128,128]{1,0:T(8,128)(2,1)S(1)} all-gather(bf16[16,128]{1,0:T(8,128)(2,1)S(1)} %bitcast.218), channel_id=1, replica_groups=mesh['dp'=4,'ctx'=2,'seq'=4] {'dp','ctx'}, dimensions={0}, use_global_device_ids=true | all-gather | bytes 36864 | tf_op jit(solution)/shard_map/all_gather | solution.py:43
  49.9 27.9 %all-gather.9.cloned.1.call-done = bf16[768,2304]{1,0:T(8,128)(2,1)} async-done(((bf16[96,2304]{1,0:T(8,128)(2,1)}), bf16[768,2304]{1,0:T(8,128)(2,1)}) %all-gather.9.cloned.1.call-update) | async-done | bytes 3538960 | tf_op jit(solution)/shard_map/all_gather | solution.py:134
  77.8 5.6 fusion.84
  88.2 31.0 %all_to_all.66 = bf16[4,128,3,768]{1,0,2,3:T(4,128)(2,1)S(1)} all-to-all(bf16[4,128,3,768]{1,0,2,3:T(4,128)(2,1)S(1)} %copy.125), channel_id=1, replica_groups=mesh['dp'=4,'ctx'=2,'seq'=4] {'seq'}, dimensions={3} | all-to-all | bytes 4718592 | tf_op jit(solution)/shard_map/all_to_all | solution.py:170
  124.1 22.5 %all-gather.13.cloned.1.call-done = bf16[4,1024,3,64]{1,3,2,0:T(8,128)(2,1)} async-done(((bf16[4,512,3,64]{1,3,2,0:T(8,128)(2,1)}), bf16[4,1024,3,64]{1,3,2,0:T(8,128)(2,1)}) %all-gather.13.cloned.1.call-update) | async-done | bytes 1572880 | tf_op jit(solution)/shard_map/all_gather | solution.py:182
  146.6 29.3 %all-gather.11.cloned.1.call-done = bf16[4,1024,3,64]{1,3,2,0:T(8,128)(2,1)} async-done(((bf16[4,512,3,64]{1,3,2,0:T(8,128)(2,1)}), bf16[4,1024,3,64]{1,3,2,0:T(8,128)(2,1)}) %all-gather.11.cloned.1.call-update) | async-done | bytes 1572880 | tf_op jit(solution)/shard_map/all_gather | solution.py:181
  175.9 43.8 %while.48 = (s32[]{:T(128)}, f32[4,512,3]{1,2,0:T(4,128)S(1)}, f32[4,512,3]{1,2,0:T(4,128)S(1)}, f32[4,512,3,64]{1,3,2,0:T(8,128)S(1)}, s32[4,1024]{1,0:T(4,128)...) while((s32[]{:T(128)}, f32[4,512,3]{1,2,0:T(4,128)S(1)}, ...), condition=%wide.region_5.6_spmd.clone, body=%wide.region_2.5_spmd.clone.sunk | while | flops 842168320 | bytes 54182116 | solution.py:85
  176.7 7.2 fusion.161
  183.9 7.7 fusion.162
  191.6 6.1 bitcast_add_fusion.9
  198.6 7.3 fusion.161
  205.9 7.5 fusion.162
  213.5 6.1 bitcast_add_fusion.9
  227.8 13.5 %all-to-all-done.1 = bf16[4,512,192]{2,0,1:T(4,128)(2,1)S(1)} async-done(((bf16[4,512,192]{2,0,1:T(4,128)(2,1)}), bf16[4,512,192]{2,0,1:T(4,128)(2,1)S(1)}, u32[]{:S(2)}, u32[]{:S(2)}) %all-to-all-start.1) | async-done | bytes 786464 | tf_op jit(solution)/shard_map/all_to_all | solution.py:206
  244.6 54.6 %all-gather.17.cloned.1.call-done = bf16[768,3072]{1,0:T(8,128)(2,1)} async-done(((bf16[96,3072]{1,0:T(8,128)(2,1)}), bf16[768,3072]{1,0:T(8,128)(2,1)}) %all-gather.17.cloned.1.call-update) | async-done | bytes 4718608 | tf_op jit(solution)/shard_map/all_gather | solution.py:134
  306.5 5.5 convolution_bitcast_fusion.1
  312.1 66.9 %all-gather.19.cloned.1.call-done = bf16[3072,768]{1,0:T(8,128)(2,1)} async-done(((bf16[384,768]{1,0:T(8,128)(2,1)}), bf16[3072,768]{1,0:T(8,128)(2,1)}) %all-gather.19.cloned.1.call-update) | async-done | bytes 4718608 | tf_op jit(solution)/shard_map/all_gather | solution.py:134
  379.0 11.1 fusion.120
  390.0 7.0 multiply_reduce_fusion
  402.2 6.4 convolution_bitcast_fusion
  418.5 6.4 all-to-all-done.2
  428.4 33.8 %while.49 = (s32[]{:T(128)}, f32[4,512,3,64]{1,3,2,0:T(8,128)}, bf16[4,1024,3,64]{1,3,2,0:T(8,128)(2,1)S(1)}, s32[4,1024]{1,0:T(4,128)S(1)}, s32[4,512]{1,0:T(4,...) while((s32[]{:T(128)}, f32[4,512,3,64]{1,3,2,0:T(8,128)}, ...), condition=%wide.region_12.13_spmd.clone, body=%wide.region_11.12_spmd.clone.sunk | while | flops 1229062144 | bytes 34440908 | solution.py:85
  429.4 6.7 fusion.170
  436.1 9.4 bitcast_add_fusion.10
  446.2 6.3 fusion.170
  452.6 9.6 bitcast_add_fusion.10
  469.7 53.3 %while.50 = (s32[]{:T(128)}, f32[4,512,3,64]{1,3,2,0:T(8,128)}, f32[4,512,3,64]{1,3,2,0:T(8,128)}, bf16[4,1024,3,64]{1,3,2,0:T(8,128)(2,1)}, s32[4,512]{1,0:T(4,...) while((s32[]{:T(128)}, f32[4,512,3,64]{1,3,2,0:T(8,128)}, ...), condition=%wide.region_14.15_spmd.clone, body=%wide.region_13.14_spmd.clone.sunk | while | flops 1645084672 | bytes 58418936 | solution.py:85
  471.3 7.6 fusion.179
  478.9 9.4 bitcast_add_fusion.11
  488.4 7.7 bitcast_add_fusion.12
  497.6 7.6 fusion.179
  505.2 9.6 bitcast_add_fusion.11
  514.9 8.1 bitcast_add_fusion.12
  534.9 35.7 %all-to-all-done.3 = bf16[4,512,3,192]{3,0,2,1:T(4,128)(2,1)S(1)} async-done(((bf16[4,512,3,192]{3,0,2,1:T(4,128)(2,1)}), bf16[4,512,3,192]{3,0,2,1:T(4,128)(2,1)S(1)}, u32[]{:S(2)}, u32[]{:S(2)}) %all-to-all-start.3) | async-done | bytes 2359328 | tf_op jit(solution)/shard_map/all_to_all | solution.py:331
  572.2 4.8 copy.139
  577.0 5.4 fusion.113
  593.0 9.1 add_convert_fusion.1
  602.1 34.2 %reduce-scatter.7.cloned.1.call-done = bf16[24,768]{1,0:T(8,128)(2,1)} async-done(((bf16[768,768]{1,0:T(8,128)(2,1)}), bf16[24,768]{1,0:T(8,128)(2,1)}) %reduce-scatter.7.cloned.1.call-update) | async-done | bytes 36880 | tf_op jit(solution)/shard_map/reduce_scatter | solution.py:76
  636.3 5.7 all_gather.63
  646.1 114.6 %all-reduce.3.cloned.1.call-done = bf16[256,128]{1,0:T(8,128)(2,1)} async-done(((bf16[256,128]{1,0:T(8,128)(2,1)}), bf16[256,128]{1,0:T(8,128)(2,1)}) %all-reduce.3.cloned.1.call-update) | async-done | bytes 65552
  761.4 6.3 all_gather.61
  768.9 106.2 %reduce-scatter.9.cloned.1.call-done = bf16[24,3072]{1,0:T(8,128)(2,1)} async-done(((bf16[768,3072]{1,0:T(8,128)(2,1)}), bf16[24,3072]{1,0:T(8,128)(2,1)}) %reduce-scatter.9.cloned.1.call-update) | async-done | bytes 147472 | tf_op jit(solution)/shard_map/reduce_scatter | solution.py:76
  875.1 7.7 all_gather.64
  884.0 103.1 %reduce-scatter.11.cloned.1.call-done = bf16[96,768]{1,0:T(8,128)(2,1)} async-done(((bf16[3072,768]{1,0:T(8,128)(2,1)}), bf16[96,768]{1,0:T(8,128)(2,1)}) %reduce-scatter.11.cloned.1.call-update) | async-done | bytes 147472 | tf_op jit(solution)/shard_map/reduce_scatter | solution.py:76
  987.1 7.5 all_gather.65
  995.8 99.1 %reduce-scatter.5.cloned.1.call-done = bf16[24,2304]{1,0:T(8,128)(2,1)} async-done(((bf16[768,2304]{1,0:T(8,128)(2,1)}), bf16[24,2304]{1,0:T(8,128)(2,1)}) %reduce-scatter.5.cloned.1.call-update) | async-done | bytes 110608 | tf_op jit(solution)/shard_map/reduce_scatter | solution.py:76
  1094.9 7.0 all_gather.62
  (230 shorter events, 96.9 us)
Async XLA Ops:
  7.2 42.3 %copy-start.4 = (bf16[4,128,768]{2,1,0:T(8,128)(2,1)S(1)}, bf16[4,128,768]{2,1,0:T(8,128)(2,1)}, u32[]{:S(2)}) copy-start(bf16[4,128,768]{2,1,0:T(8,128)(2,1)} %param.22) | copy-start | bytes 2359300
  7.2 70.6 %all-gather.9.cloned.1.call-start = ((), (), s32[]{:S(2)}) async-start(), calls=%async_computation.8 | async-start | bytes 3981312 | tf_op jit(solution)/shard_map/all_gather | solution.py:134
  7.9 138.7 %all-gather.13.cloned.1.call-start = ((), (), s32[]{:S(2)}) async-start(), calls=%async_computation.10 | async-start | bytes 2359296 | tf_op jit(solution)/shard_map/all_gather | solution.py:182
  48.0 29.7 %copy-start.18 = (f32[768]{0:T(1024)}, f32[768]{0:T(1024)S(1)}, u32[]{:S(2)}) copy-start(f32[768]{0:T(1024)S(1)} %reshape.268) | copy-start | bytes 9220
  48.1 29.6 %copy-start.34 = (f32[768]{0:T(1024)}, f32[768]{0:T(1024)S(1)}, u32[]{:S(2)}) copy-start(f32[768]{0:T(1024)S(1)} %reshape.269) | copy-start | bytes 9220
  49.5 28.3 %copy-start.20 = (f32[4,128]{1,0:T(4,128)}, f32[4,128]{1,0:T(4,128)S(1)}, u32[]{:S(2)}) copy-start(f32[4,128]{1,0:T(4,128)S(1)} %broadcast_multiply_fusion.1) | copy-start | bytes 6148
  49.8 27.9 %copy-start.22 = (f32[4,128]{1,0:T(4,128)}, f32[4,128]{1,0:T(4,128)S(1)}, u32[]{:S(2)}) copy-start(f32[4,128]{1,0:T(4,128)S(1)} %fusion.99) | copy-start | bytes 6148
  49.9 27.9 %copy-start.24 = (f32[4,128]{1,0:T(4,128)}, f32[4,128]{1,0:T(4,128)S(1)}, u32[]{:S(2)}) copy-start(f32[4,128]{1,0:T(4,128)S(1)} %fusion.111) | copy-start | bytes 6148
  121.4 2.6 copy-start.36
  121.4 54.5 %all-gather.11.cloned.1.call-start = ((), (), s32[]{:S(2)}) async-start(), calls=%async_computation.9 | async-start | bytes 2359296 | tf_op jit(solution)/shard_map/all_gather | solution.py:181
  122.2 119.9 %all-gather.15.cloned.1.call-start = ((), (), s32[]{:S(2)}) async-start(), calls=%async_computation.11 | async-start | bytes 1327104 | tf_op jit(solution)/shard_map/all_gather | solution.py:134
  122.7 176.5 %all-gather.17.cloned.1.call-start = ((), (), s32[]{:S(2)}) async-start(), calls=%async_computation.12 | async-start | bytes 5308416 | tf_op jit(solution)/shard_map/all_gather | solution.py:134
  123.3 255.6 %all-gather.19.cloned.1.call-start = ((), (), s32[]{:S(2)}) async-start(), calls=%async_computation.13 | async-start | bytes 5308416 | tf_op jit(solution)/shard_map/all_gather | solution.py:134
  183.9 7.7 copy-start.39
  205.9 7.6 copy-start.39
  219.7 3.6 copy-start
  219.7 3.6 copy-start.12
  223.4 17.9 %all-to-all-start.1 = ((bf16[4,512,192]{2,0,1:T(4,128)(2,1)}), bf16[4,512,192]{2,0,1:T(4,128)(2,1)S(1)}, u32[]{:S(2)}, u32[]{:S(2)}) async-start(bf16[4,512,192]{2,0,1:T(4,128)(2,1)} %copy.128), calls=%async_computation.1 | async-start | bytes 2097152 | tf_op jit(solution)/shard_map/all_to_all | solution.py:206
  226.9 242.9 %all-gather.21.cloned.1.call-start = ((), (), s32[]{:S(2)}) async-start(), calls=%async_computation.14 | async-start | bytes 2359296 | tf_op jit(solution)/shard_map/all_gather | solution.py:295
  227.5 151.4 %copy-start.29 = (f32[3072]{0:T(1024)}, f32[3072]{0:T(1024)S(1)}, u32[]{:S(2)}) copy-start(f32[3072]{0:T(1024)S(1)} %reshape.273) | copy-start | bytes 36868
  244.3 157.9 %copy-start.6 = (f32[4,128,768]{2,1,0:T(8,128)}, f32[4,128,768]{2,1,0:T(8,128)S(1)}, u32[]{:S(2)}) copy-start(f32[4,128,768]{2,1,0:T(8,128)S(1)} %get-tuple-element.780) | copy-start | bytes 4718596
  244.6 61.9 %copy-start.14 = (bf16[4,128,768]{2,1,0:T(8,128)(2,1)S(1)}, bf16[4,128,768]{2,1,0:T(8,128)(2,1)}, u32[]{:S(2)}) copy-start(bf16[4,128,768]{2,1,0:T(8,128)(2,1)} %param.37) | copy-start | bytes 2359300
  303.9 2.6 copy-start.40
  390.0 7.1 copy-start.41
  409.9 15.1 %all-to-all-start.2 = ((bf16[4,128,768]{1,0,2:T(4,128)(2,1)}), bf16[4,128,768]{1,0,2:T(4,128)(2,1)S(1)}, u32[]{:S(2)}, u32[]{:S(2)}) async-start(bf16[4,128,768]{1,0,2:T(4,128)(2,1)} %copy.134), calls=%async_computation.2 | async-start | bytes 1572864 | tf_op jit(solution)/shard_map/all_to_all | solution.py:252
  413.4 56.4 %all-gather.23.cloned.1.call-start = ((), (), s32[]{:S(2)}) async-start(), calls=%async_computation.15 | async-start | bytes 2359296 | tf_op jit(solution)/shard_map/all_gather | solution.py:296
  426.0 2.4 copy-start.2
  462.2 7.6 copy-start.3
  471.3 7.6 copy-start.10
  497.6 7.6 copy-start.10
  529.8 4.7 copy-start.33
  529.8 4.7 copy-start.38
  529.8 4.8 copy-start.37
  529.8 4.9 copy-start.32
  529.8 4.9 copy-start.31
  529.8 40.7 %all-to-all-start.3 = ((bf16[4,512,3,192]{3,0,2,1:T(4,128)(2,1)}), bf16[4,512,3,192]{3,0,2,1:T(4,128)(2,1)S(1)}, u32[]{:S(2)}, u32[]{:S(2)}) async-start(bf16[4,512,3,192]{3,0,2,1:T(4,128)(2,1)} %copy.137), calls=%async_computation.3 | async-start | bytes 6291456 | tf_op jit(solution)/shard_map/all_to_all | solution.py:331
  533.7 102.6 %reduce-scatter.7.cloned.1.call-start = ((), (), s32[]{:S(2)}) async-start(), calls=%async_computation.17 | async-start | bytes 1216512 | tf_op jit(solution)/shard_map/reduce_scatter | solution.py:76
  534.4 226.3 %all-reduce.3.cloned.1.call-start = ((), (), s32[]{:S(2)}) async-start(), calls=%async_computation.20 | async-start | bytes 131072
  572.2 4.8 copy-start.5
  572.2 4.8 copy-start.19
  572.2 4.8 copy-start.21
  577.0 5.5 copy-start.23
  577.0 5.5 copy-start.25
  586.0 289.1 %reduce-scatter.9.cloned.1.call-start = ((), (), s32[]{:S(2)}) async-start(), calls=%async_computation.18 | async-start | bytes 4866048 | tf_op jit(solution)/shard_map/reduce_scatter | solution.py:76
  586.8 400.4 %reduce-scatter.11.cloned.1.call-start = ((), (), s32[]{:S(2)}) async-start(), calls=%async_computation.19 | async-start | bytes 4866048 | tf_op jit(solution)/shard_map/reduce_scatter | solution.py:76
  587.3 507.5 %reduce-scatter.5.cloned.1.call-start = ((), (), s32[]{:S(2)}) async-start(), calls=%async_computation.16 | async-start | bytes 3649536 | tf_op jit(solution)/shard_map/reduce_scatter | solution.py:76
  593.0 49.7 %copy-start.15 = (bf16[4,128,768]{2,1,0:T(8,128)(2,1)S(1)}, bf16[4,128,768]{2,1,0:T(8,128)(2,1)}, u32[]{:S(2)}) copy-start(bf16[4,128,768]{2,1,0:T(8,128)(2,1)} %param.37) | copy-start | bytes 2359300
  593.0 49.7 %copy-start.27 = (f32[4,128]{1,0:T(4,128)S(1)}, f32[4,128]{1,0:T(4,128)}, u32[]{:S(2)}) copy-start(f32[4,128]{1,0:T(4,128)} %copy-done.26) | copy-start | bytes 6148
  (12 other events, 17.2 us)
Sparse Core Ops, SparseCore 0:
  10.2 67.5 all-gather.8
  121.5 25.0 all-gather.12
  148.7 27.1 all-gather.10
  178.0 41.1 all-gather.14
  221.2 78.0 all-gather.16
  301.2 77.6 all-gather.18
  381.1 25.5 all-gather.20
  428.2 24.6 all-gather.22
  540.2 96.0 reduce-scatter.6
  642.3 118.4 all-reduce.2
  766.2 108.8 reduce-scatter.8
  880.5 106.6 reduce-scatter.10
  992.6 102.2 reduce-scatter.4
